TPU v7x, 32 devices: a whole 2x2x4 slice. The times are simulated.
32 devices in a mesh: ctx: 2 (over x), req: 4 (over y, core), mp: 4 (over z).
Axes of the slice: x: 2, y: 2, z: 4, core: 2. Of those that a mesh axis runs over, the one named last changes fastest.
Arguments:
- activations: bfloat16 [4, 256, 8192], P('req', 'ctx', 'mp'), may hold values from -6 to 6
- query_base: bfloat16 [4, 256, 8192], P('req', 'ctx', 'mp'), may hold values from -9 to 9
- key_base: bfloat16 [4, 256, 1024], P('req', 'ctx', 'mp'), may hold values from -9 to 9
- plain_value_rows: bfloat16 [4, 256, 1024], P('req', 'ctx', 'mp'), may hold values from -6 to 6
- query_down: bfloat16 [8, 64, 8192], P('req', 'ctx', 'mp'), may hold values from -0.0625 to 0.0625
- query_up: bfloat16 [8, 64, 8192], P('req', 'ctx', 'mp'), may hold values from -0.75 to 0.75
- value_down: bfloat16 [8, 64, 8192], P('req', 'ctx', 'mp'), may hold values from -0.0625 to 0.0625
- value_raise_factor: bfloat16 [8, 64, 1024], P('req', 'ctx', 'mp'), may hold values from -0.75 to 0.75
- member_lists: int32 [4, 2], P('req'), may hold values from 0 to 7
- prompt_lengths: int32 [4], P('req'), may hold values from 32 to 256, as said below
Outputs:
- attended: bfloat16 [2, 4, 256, 8192], P(None, 'req', 'ctx', 'mp')
Inputs may be any that keep to these rules, and one draw needn't show every extreme that they name: `prompt_lengths`: at least one prompt has all 256 positions live.
All inputs are finite; a program needn't handle non-finite values.
Results may differ from a plain program's by a relative error of at most 0.008.
Values may be sent and summed in bfloat16 or wider, within the bound.
No kernel may reach another device: no remote copies, remote signals or barrier semaphores. Data moves between devices by JAX's collectives and lax.ppermute only.
A program may use at most 64 MiB of HBM per device.

v0:
```python
import math

import jax
import jax.numpy as jnp
from jax import lax
from jax.sharding import PartitionSpec as P

HEAD_SIZE = 128


def block_rows(total_rows):
    if total_rows <= 512:
        return total_rows
    for candidate in range(512, 0, -1):
        if total_rows % candidate == 0:
            return candidate
    return total_rows


def select_members(factor_set, member_ids, member_count):
    onehot = (member_ids[:, None] == jnp.arange(member_count, dtype=jnp.int32)[None, :]).astype(
        jnp.bfloat16
    )
    return tuple(
        (
            jnp.einsum("sm,mkc->skc", onehot, factor, preferred_element_type=jnp.float32).astype(
                jnp.bfloat16
            )
            for factor in factor_set
        )
    )


def per_device(
    activations,
    query_base,
    key_base,
    plain_value_rows,
    query_down,
    query_up,
    value_down,
    value_raise_factor,
    member_lists,
    prompt_lengths,
):
    row_count = activations.shape[1]
    member_count = query_down.shape[0] * lax.axis_size("req")
    member_ids = member_lists[0]
    full_rank = (
        lax.all_gather(query_down, "ctx", axis=1, tiled=True),
        lax.all_gather(query_up, "ctx", axis=1, tiled=True),
        lax.all_gather(value_down, "ctx", axis=1, tiled=True),
        lax.all_gather(value_raise_factor, "ctx", axis=1, tiled=True),
    )
    all_members = (
        lax.all_gather(full_rank[0], "req", axis=0, tiled=True),
        lax.all_gather(full_rank[1], "req", axis=0, tiled=True),
        lax.all_gather(full_rank[2], "req", axis=0, tiled=True),
        lax.all_gather(full_rank[3], "req", axis=0, tiled=True),
    )
    chosen = select_members(all_members, member_ids, member_count)
    down_query, up_query, down_value, up_value = chosen
    tokens = activations[0]
    rank_query = jnp.einsum("rd,skd->rsk", tokens, down_query, preferred_element_type=jnp.float32)
    rank_value = jnp.einsum("rd,skd->rsk", tokens, down_value, preferred_element_type=jnp.float32)
    rank_query, rank_value = lax.psum((rank_query, rank_value), "mp")
    rank_query = rank_query.astype(jnp.bfloat16)
    rank_value = rank_value.astype(jnp.bfloat16)
    query_matrix = (
        query_base[0][:, None, :]
        + jnp.einsum("rsk,skc->rsc", rank_query, up_query, preferred_element_type=jnp.float32)
    ).astype(jnp.bfloat16)
    slot_count = query_matrix.shape[1]
    rank_width = rank_value.shape[2]
    group_count = key_base.shape[2] // HEAD_SIZE
    group_portion = query_matrix.shape[2] // (group_count * HEAD_SIZE)
    grouped = query_matrix.reshape(row_count, slot_count, group_count, group_portion, HEAD_SIZE)
    rows_of_keys = key_base[0]
    positions = lax.axis_index("ctx") * row_count + jnp.arange(row_count, dtype=jnp.int32)
    live_length = prompt_lengths[0]
    inverse = 1.0 / math.sqrt(HEAD_SIZE)

    def update(running, key_block, value_block, key_start):
        run_max, run_total, accumulated = running
        block_length = key_block.shape[0]
        heads_of_keys = key_block.reshape(block_length, group_count, HEAD_SIZE)
        heads_of_values = value_block.reshape(block_length, slot_count, group_count, HEAD_SIZE)
        scores = (
            jnp.einsum(
                "rsgjd,kgd->sgjrk", grouped, heads_of_keys, preferred_element_type=jnp.float32
            )
            * inverse
        )
        key_positions = key_start + jnp.arange(block_length, dtype=jnp.int32)
        visible = (key_positions[None, :] <= positions[:, None]) & (
            key_positions[None, :] < live_length
        )
        masked = jnp.where(visible, scores, -1e30)
        new_max = jnp.maximum(run_max, jnp.max(masked, axis=-1))
        weights = jnp.where(visible, jnp.exp(masked - new_max[..., None]), 0.0)
        factor = jnp.exp(run_max - new_max)
        new_total = run_total * factor + jnp.sum(weights, axis=-1)
        new_accumulated = accumulated * factor[..., None] + jnp.einsum(
            "sgjrk,ksgd->sgjrd",
            weights.astype(jnp.bfloat16),
            heads_of_values,
            preferred_element_type=jnp.float32,
        )
        return (new_max, new_total, new_accumulated)

    initial = (
        jnp.full((slot_count, group_count, group_portion, row_count), -1e30, jnp.float32),
        jnp.zeros((slot_count, group_count, group_portion, row_count), jnp.float32),
        jnp.zeros((slot_count, group_count, group_portion, row_count, HEAD_SIZE), jnp.float32),
    )
    base_rows = plain_value_rows[0]
    piece_rows = base_rows.shape[0]
    ranks = rank_value.reshape(row_count, slot_count * rank_width).reshape(
        piece_rows, slot_count, rank_width
    )
    built = (
        base_rows[:, None, :]
        + jnp.einsum("rsk,skc->rsc", ranks, up_value, preferred_element_type=jnp.float32)
    ).astype(jnp.bfloat16)
    packed = built.reshape(piece_rows, slot_count * group_count * HEAD_SIZE)
    key_piece = lax.all_gather(rows_of_keys, "ctx", axis=0, tiled=True)
    value_piece = lax.all_gather(packed, "ctx", axis=0, tiled=True)
    first_row = jnp.int32(0)
    piece_rows = key_piece.shape[0]
    step_rows = block_rows(piece_rows)

    def advance(block_index, current):
        offset = block_index * step_rows
        key_block = lax.dynamic_slice_in_dim(key_piece, offset, step_rows, 0)
        value_block = lax.dynamic_slice_in_dim(value_piece, offset, step_rows, 0)
        key_start = first_row + offset
        return update(current, key_block, value_block, key_start)

    run_max, run_total, accumulated = lax.fori_loop(0, piece_rows // step_rows, advance, initial)
    result = accumulated / run_total[..., None]
    result = (
        jnp.transpose(result, (0, 3, 1, 2, 4))
        .reshape(slot_count, row_count, group_count * group_portion * HEAD_SIZE)
        .astype(jnp.bfloat16)
    )
    return result[:, None]


def solution(mesh):
    in_specs = (
        P("req", "ctx", "mp"),
        P("req", "ctx", "mp"),
        P("req", "ctx", "mp"),
        P("req", "ctx", "mp"),
        P("req", "ctx", "mp"),
        P("req", "ctx", "mp"),
        P("req", "ctx", "mp"),
        P("req", "ctx", "mp"),
        P("req", None),
        P("req"),
    )
    out_specs = P(None, "req", "ctx", "mp")
    return jax.shard_map(
        per_device, mesh=mesh, in_specs=in_specs, out_specs=out_specs, check_vma=False
    )
```

profile of v0, /device:TPU:0, one launch (start us, length us, event | category | flops | bytes accessed | tf_op | source)
XLA Modules:
  0.0 111.7 jit_solution(13145723315272196515)
XLA Ops:
  6.5 0.0 copy-start
  6.5 0.0 copy-start.2
  6.5 0.0 copy-start.1
  6.5 0.0 all-gather.9.cloned.1.call-start
  6.5 12.0 %all_gather.37 = bf16[2,64,2048]{2,1,0:T(8,128)(2,1)} all-gather(bf16[2,32,2048]{2,1,0:T(8,128)(2,1)} %param.16), channel_id=1, replica_groups=mesh['ctx'=2,'req'=4,'mp'=4] {'ctx'}, dimensions={1}, use_global_device_ids=true | all-gather | bytes 786432 | tf_op jit(solution)/shard_map/all_gather | solution.py:52
  18.6 0.0 all-gather.9.cloned.1.call-update
  18.6 0.0 all-gather.7.cloned.1.call-start
  18.6 8.5 %all_gather.32 = bf16[2,64,2048]{2,1,0:T(8,128)(2,1)} all-gather(bf16[2,32,2048]{2,1,0:T(8,128)(2,1)} %param.14), channel_id=1, replica_groups=mesh['ctx'=2,'req'=4,'mp'=4] {'ctx'}, dimensions={1}, use_global_device_ids=true | all-gather | bytes 786432 | tf_op jit(solution)/shard_map/all_gather | solution.py:50
  27.1 0.0 all-gather.7.cloned.1.call-update
  27.1 0.0 all-gather.5.cloned.1.call-start
  27.2 0.0 copy-done.2
  27.2 7.9 %all_gather.30 = bf16[2,64,2048]{2,1,0:T(8,128)(2,1)} all-gather(bf16[2,32,2048]{2,1,0:T(8,128)(2,1)S(1)} %copy-done.2), channel_id=1, replica_groups=mesh['ctx'=2,'req'=4,'mp'=4] {'ctx'}, dimensions={1}, use_global_device_ids=true | all-gather | bytes 786432 | tf_op jit(solution)/shard_map/all_gather | solution.py:51
  35.0 0.0 copy-start.4
  35.0 0.0 copy-start.3
  35.0 0.0 all-gather.5.cloned.1.call-update
  35.1 0.0 copy-done.1
  35.1 0.0 copy-start.5
  35.1 0.0 copy-start.6
  35.1 0.1 bitcast_convert_fusion
  35.2 0.3 copy.27
  36.2 0.0 copy-done.4
  36.2 0.1 copy.32
  36.3 0.0 copy-done.3
  36.4 0.1 copy.36
  36.5 0.0 copy-done.5
  36.5 4.6 %all_gather.35 = bf16[2,64,256]{2,1,0:T(8,128)(2,1)S(1)} all-gather(bf16[2,32,256]{2,1,0:T(8,128)(2,1)S(1)} %copy-done.5), channel_id=1, replica_groups=mesh['ctx'=2,'req'=4,'mp'=4] {'ctx'}, dimensions={1}, use_global_device_ids=true | all-gather | bytes 98304 | tf_op jit(solution)/shard_map/all_gather | solution.py:53
  41.0 5.0 %all-gather = bf16[1,256,256]{1,2,0:T(8,128)(2,1)S(1)} all-gather(bf16[1,128,256]{1,2,0:T(8,128)(2,1)S(1)} %copy.32), channel_id=2, replica_groups=mesh['ctx'=2,'req'=4,'mp'=4] {'ctx'}, dimensions={1}, use_global_device_ids=true | all-gather | bytes 196608 | tf_op jit(solution)/shard_map/all_gather | solution.py:126
  46.0 6.0 %all_gather.36 = bf16[8,64,256]{2,1,0:T(8,128)(2,1)S(1)} all-gather(bf16[2,64,256]{2,1,0:T(8,128)(2,1)S(1)} %all_gather.35), channel_id=1, replica_groups=mesh['ctx'=2,'req'=4,'mp'=4] {'req'}, dimensions={0}, use_global_device_ids=true | all-gather | bytes 327680 | tf_op jit(solution)/shard_map/all_gather | solution.py:59
  52.0 0.1 fusion.25
  52.1 0.0 copy-done.6
  52.1 0.3 convolution_convert_fusion.3
  52.4 0.0 all-gather.9.cloned.1.call-done
  52.5 3.1 %convolution_convert_fusion = bf16[2,64,2048]{2,0,1:T(2,128)(2,1)S(1)} fusion(bf16[8,64,2048]{2,1,0:T(8,128)(2,1)} %all-gather.9.cloned.1.call-done, s32[2]{0:T(128)S(1)} %bitcast.86), kind=kOutput, calls=%fused_computation.10 | convolution fusion | flops 4456464 | bytes 2621448 | tf_op jit(solution)/shard_map/sm,mkc->skc/dot_general | solution.py:26
  55.6 0.0 copy-done
  55.6 0.4 convolution_bitcast_fusion.2
  56.0 9.8 %all-gather.7.cloned.1.call-done = bf16[8,64,2048]{2,1,0:T(8,128)(2,1)} async-done(((bf16[2,64,2048]{2,1,0:T(8,128)(2,1)}), bf16[8,64,2048]{2,1,0:T(8,128)(2,1)}) %all-gather.7.cloned.1.call-update) | async-done | bytes 2097168 | tf_op jit(solution)/shard_map/all_gather | solution.py:56
  65.8 3.1 %convolution_convert_fusion.1 = bf16[2,64,2048]{2,0,1:T(2,128)(2,1)S(1)} fusion(bf16[8,64,2048]{2,1,0:T(8,128)(2,1)} %all-gather.7.cloned.1.call-done, s32[2]{0:T(128)S(1)} %bitcast.87), kind=kOutput, calls=%fused_computation.11 | convolution fusion | flops 4456464 | bytes 2621448 | tf_op jit(solution)/shard_map/sm,mkc->skc/dot_general | solution.py:26
  68.9 0.4 convolution_bitcast_fusion.3
  69.3 21.2 %all-reduce.2 = (bf16[128,2,64]{0,2,1:T(8,128)(2,1)S(1)}, bf16[128,2,64]{0,2,1:T(8,128)(2,1)S(1)}) all-reduce(f32[128,2,64]{0,2,1:T(8,128)S(1)} %convolution_bitcast_fusion.2, f32[128,2,64]{0,2,1:T(8,128)S(1)} %convolution_bitcast_fusion.3), channel_id=1, replica_groups=mesh['ctx'=2,'req'=4,'mp'=4] {'mp'}, use_global_device_ids=true, to_apply=%region_2.3 | all-reduce | flops 32768 | bytes 196608 | tf_op jit(solution)/shard_map/psum | solution.py:66
  90.5 0.0 all-gather.5.cloned.1.call-done
  90.5 3.1 %convolution_convert_fusion.2 = bf16[2,64,2048]{2,0,1:T(2,128)(2,1)S(1)} fusion(bf16[8,64,2048]{2,1,0:T(8,128)(2,1)} %all-gather.5.cloned.1.call-done, s32[2]{0:T(128)S(1)} %bitcast.88), kind=kOutput, calls=%fused_computation.12 | convolution fusion | flops 4456464 | bytes 2621448 | tf_op jit(solution)/shard_map/sm,mkc->skc/dot_general | solution.py:26
  93.7 0.6 fusion.5
  94.2 1.0 bitcast_reduce_fusion
  95.3 1.7 %fusion.2 = (f32[2,2,8,128]{3,2,0,1:T(8,128)S(1)}, bf16[2,2,8,128,256]{4,3,2,0,1:T(8,128)(2,1)S(1)}) fusion(f32[2,128,2,8,256]{4,1,3,2,0:T(8,128)S(1)} %get-tuple-element.40, f32[2,2,8,128]{3,2,0,1:T(8,128)S(1)} %get-tuple-element.28, pred[128,256]{1,0:T(8,128)(4,1)S(1)} %fusion.25), kind=kLoop, calls=%fused_computation.5 | loop fusion | flops 6287360 | bytes 6356992 | tf_op jit(solution)/shard_map/while/body/eval_jaxpr/reduce_sum | solution.py:102
  97.0 0.2 fusion.16
  97.3 5.8 %all_gather.39 = bf16[256,512]{0,1:T(8,128)(2,1)S(1)} all-gather(bf16[128,512]{0,1:T(8,128)(2,1)S(1)} %bitcast.83), channel_id=1, replica_groups=mesh['ctx'=2,'req'=4,'mp'=4] {'ctx'}, dimensions={0}, use_global_device_ids=true | all-gather | bytes 393216 | tf_op jit(solution)/shard_map/all_gather | solution.py:127
  103.1 0.8 fusion.7
  103.9 1.3 %copy.43 = bf16[2,1,128,2048]{3,2,1,0:T(8,128)(2,1)} copy(bf16[2,1,128,2048]{2,3,0,1:T(8,128)(2,1)S(1)} %bitcast.81) | data formatting | bytes 2097152 | tf_op jit(solution)/shard_map/convert_element_type | solution.py:144
  (5 shorter events, 0.0 us)
Async XLA Ops:
  6.5 49.1 %copy-start = (bf16[1,128,2048]{2,1,0:T(8,128)(2,1)S(1)}, bf16[1,128,2048]{2,1,0:T(8,128)(2,1)}, u32[]{:S(2)}) copy-start(bf16[1,128,2048]{2,1,0:T(8,128)(2,1)} %param.10) | copy-start | bytes 1572868
  6.5 20.6 %copy-start.2 = (bf16[2,32,2048]{2,1,0:T(8,128)(2,1)S(1)}, bf16[2,32,2048]{2,1,0:T(8,128)(2,1)}, u32[]{:S(2)}) copy-start(bf16[2,32,2048]{2,1,0:T(8,128)(2,1)} %param.15) | copy-start | bytes 786436
  6.5 28.5 %copy-start.1 = (bf16[1,128,2048]{2,1,0:T(8,128)(2,1)S(1)}, bf16[1,128,2048]{2,1,0:T(8,128)(2,1)}, u32[]{:S(2)}) copy-start(bf16[1,128,2048]{2,1,0:T(8,128)(2,1)} %param.11) | copy-start | bytes 1572868
  6.5 45.9 %all-gather.9.cloned.1.call-start = ((), (), s32[]{:S(2)}) async-start(), calls=%async_computation.2 | async-start | bytes 2621440 | tf_op jit(solution)/shard_map/all_gather | solution.py:58
  18.6 47.2 %all-gather.7.cloned.1.call-start = ((), (), s32[]{:S(2)}) async-start(), calls=%async_computation.1 | async-start | bytes 2621440 | tf_op jit(solution)/shard_map/all_gather | solution.py:56
  27.1 63.4 %all-gather.5.cloned.1.call-start = ((), (), s32[]{:S(2)}) async-start(), calls=%async_computation | async-start | bytes 2621440 | tf_op jit(solution)/shard_map/all_gather | solution.py:57
  35.0 1.2 %copy-start.4 = (bf16[1,128,256]{2,1,0:T(8,128)(2,1)S(1)}, bf16[1,128,256]{2,1,0:T(8,128)(2,1)}, u32[]{:S(2)}) copy-start(bf16[1,128,256]{2,1,0:T(8,128)(2,1)} %param.12) | copy-start | bytes 196612
  35.0 1.3 %copy-start.3 = (bf16[1,128,256]{2,1,0:T(8,128)(2,1)S(1)}, bf16[1,128,256]{2,1,0:T(8,128)(2,1)}, u32[]{:S(2)}) copy-start(bf16[1,128,256]{2,1,0:T(8,128)(2,1)} %param.13) | copy-start | bytes 196612
  35.1 1.4 %copy-start.5 = (bf16[2,32,256]{2,1,0:T(8,128)(2,1)S(1)}, bf16[2,32,256]{2,1,0:T(8,128)(2,1)}, u32[]{:S(2)}) copy-start(bf16[2,32,256]{2,1,0:T(8,128)(2,1)} %param.17) | copy-start | bytes 98308
  35.1 17.0 %copy-start.6 = (s32[1,2]{1,0:T(1,128)S(1)}, s32[1,2]{1,0:T(1,128)}, u32[]{:S(2)}) copy-start(s32[1,2]{1,0:T(1,128)} %param.18) | copy-start | bytes 28
Sparse Core Ops, SparseCore 0:
  18.7 22.8 all-gather.8
  43.2 22.5 all-gather.6
  67.4 22.5 all-gather.4
where the time goes:
time: 112 us
  blocking collectives  70.8 us (63%)
  between operations  14 us (12%)
  matrix products  13.1 us (12%)
  waiting for transfers between devices  9.9 us (9%)
  other arithmetic  1.96 us (2%)
  local copies, waits for them, and re-layouts  1.87 us (2%)
    psum x1, blocking collectives, per_device(): rank_query, rank_value = lax.psum((rank_query, rank_value), 'mp')  21.2 us
    all_gather x1, blocking collectives, per_device(): lax.all_gather(value_down, 'ctx', axis=1, tiled=True)  12 us
    all_gather x1, waiting for transfers between devices, per_device(): lax.all_gather(full_rank[0], 'req', axis=0, tiled=True)  9.81 us
    dot_general x4, matrix products, select_members(): jnp.einsum('sm,mkc->skc', onehot, factor, preferred_element_type=jnp.floa...  9.69 us
    all_gather x1, blocking collectives, per_device(): lax.all_gather(query_down, 'ctx', axis=1, tiled=True)  8.45 us
    all_gather x1, blocking collectives, per_device(): lax.all_gather(query_up, 'ctx', axis=1, tiled=True)  7.85 us
    all_gather x1, blocking collectives, per_device(): lax.all_gather(full_rank[3], 'req', axis=0, tiled=True)  6.01 us
    all_gather x1, blocking collectives, per_device(): value_piece = lax.all_gather(packed, 'ctx', axis=0, tiled=True)  5.77 us
  transfers between devices with their start and end apart: 3, of which 1 were waited for; matrix products, arithmetic and copies ran while one was open for 7% of the time, Pallas kernels for 0%

commit v1 on v0

--- a/solution.py
+++ b/solution.py
@@ -17,18 +17,69 @@
     return total_rows
 
 
-def select_members(factor_set, member_ids, member_count):
-    onehot = (member_ids[:, None] == jnp.arange(member_count, dtype=jnp.int32)[None, :]).astype(
-        jnp.bfloat16
+def swap(value, axis, bit):
+    size = lax.axis_size(axis)
+    return lax.ppermute(value, axis, [(i, i ^ bit) for i in range(size)])
+
+
+def ctx_gather(mine, dim, ordered):
+    if lax.axis_size("ctx") == 2:
+        other = swap(mine, "ctx", 1)
+        if not ordered:
+            return jnp.concatenate([mine, other], axis=dim)
+        first = lax.axis_index("ctx") == 0
+        low = jnp.where(first, mine, other)
+        high = jnp.where(first, other, mine)
+        return jnp.concatenate([low, high], axis=dim)
+    return lax.all_gather(mine, "ctx", axis=dim, tiled=True)
+
+
+def mp_sum(values):
+    size = lax.axis_size("mp")
+    if size & (size - 1):
+        return lax.psum(values, "mp")
+    bit = 1
+    while bit < size:
+        values = jax.tree.map(lambda a, b: a + b, values, swap(values, "mp", bit))
+        bit *= 2
+    return values
+
+
+def select_members(factor_set, member_ids, member_lists):
+    local_count = factor_set[0].shape[0]
+    req_size = lax.axis_size("req")
+    if req_size != 4:
+        everything = [lax.all_gather(f, "req", axis=0, tiled=True) for f in factor_set]
+        return [
+            jnp.stack([lax.dynamic_index_in_dim(f, m, 0, keepdims=False) for m in member_ids])
+            for f in everything
+        ]
+    req = lax.axis_index("req")
+    core = req % 2
+    row = req // 2
+    row_span = 2 * local_count
+    partners = swap(tuple(factor_set), "req", 1)
+    far_ids = swap(member_lists, "req", 2)[0]
+
+    def pick(own, partner, index):
+        mine = lax.dynamic_index_in_dim(own, index % local_count, 0, keepdims=False)
+        theirs = lax.dynamic_index_in_dim(partner, index % local_count, 0, keepdims=False)
+        return jnp.where(index // local_count == core, mine, theirs)
+
+    outgoing = tuple(
+        jnp.stack([pick(own, partner, far_ids[s] % row_span) for s in range(far_ids.shape[0])])
+        for own, partner in zip(factor_set, partners)
     )
-    return tuple(
-        (
-            jnp.einsum("sm,mkc->skc", onehot, factor, preferred_element_type=jnp.float32).astype(
-                jnp.bfloat16
-            )
-            for factor in factor_set
-        )
-    )
+    incoming = swap(outgoing, "req", 2)
+    chosen = []
+    for own, partner, received in zip(factor_set, partners, incoming):
+        slots = []
+        for s in range(member_ids.shape[0]):
+            m = member_ids[s]
+            near = pick(own, partner, m % row_span)
+            slots.append(jnp.where(m // row_span == row, near, received[s]))
+        chosen.append(jnp.stack(slots))
+    return chosen
 
 
 def per_device(
@@ -44,26 +95,15 @@
     prompt_lengths,
 ):
     row_count = activations.shape[1]
-    member_count = query_down.shape[0] * lax.axis_size("req")
     member_ids = member_lists[0]
-    full_rank = (
-        lax.all_gather(query_down, "ctx", axis=1, tiled=True),
-        lax.all_gather(query_up, "ctx", axis=1, tiled=True),
-        lax.all_gather(value_down, "ctx", axis=1, tiled=True),
-        lax.all_gather(value_raise_factor, "ctx", axis=1, tiled=True),
+    halves = select_members(
+        (query_down, value_down, query_up, value_raise_factor), member_ids, member_lists
     )
-    all_members = (
-        lax.all_gather(full_rank[0], "req", axis=0, tiled=True),
-        lax.all_gather(full_rank[1], "req", axis=0, tiled=True),
-        lax.all_gather(full_rank[2], "req", axis=0, tiled=True),
-        lax.all_gather(full_rank[3], "req", axis=0, tiled=True),
-    )
-    chosen = select_members(all_members, member_ids, member_count)
-    down_query, up_query, down_value, up_value = chosen
+    down_query, down_value, up_query, up_value = [ctx_gather(h, 1, False) for h in halves]
     tokens = activations[0]
     rank_query = jnp.einsum("rd,skd->rsk", tokens, down_query, preferred_element_type=jnp.float32)
     rank_value = jnp.einsum("rd,skd->rsk", tokens, down_value, preferred_element_type=jnp.float32)
-    rank_query, rank_value = lax.psum((rank_query, rank_value), "mp")
+    rank_query, rank_value = mp_sum((rank_query, rank_value))
     rank_query = rank_query.astype(jnp.bfloat16)
     rank_value = rank_value.astype(jnp.bfloat16)
     query_matrix = (
@@ -71,7 +111,6 @@
         + jnp.einsum("rsk,skc->rsc", rank_query, up_query, preferred_element_type=jnp.float32)
     ).astype(jnp.bfloat16)
     slot_count = query_matrix.shape[1]
-    rank_width = rank_value.shape[2]
     group_count = key_base.shape[2] // HEAD_SIZE
     group_portion = query_matrix.shape[2] // (group_count * HEAD_SIZE)
     grouped = query_matrix.reshape(row_count, slot_count, group_count, group_portion, HEAD_SIZE)
@@ -114,18 +153,13 @@
         jnp.zeros((slot_count, group_count, group_portion, row_count, HEAD_SIZE), jnp.float32),
     )
     base_rows = plain_value_rows[0]
-    piece_rows = base_rows.shape[0]
-    ranks = rank_value.reshape(row_count, slot_count * rank_width).reshape(
-        piece_rows, slot_count, rank_width
-    )
     built = (
         base_rows[:, None, :]
-        + jnp.einsum("rsk,skc->rsc", ranks, up_value, preferred_element_type=jnp.float32)
+        + jnp.einsum("rsk,skc->rsc", rank_value, up_value, preferred_element_type=jnp.float32)
     ).astype(jnp.bfloat16)
-    packed = built.reshape(piece_rows, slot_count * group_count * HEAD_SIZE)
-    key_piece = lax.all_gather(rows_of_keys, "ctx", axis=0, tiled=True)
-    value_piece = lax.all_gather(packed, "ctx", axis=0, tiled=True)
-    first_row = jnp.int32(0)
+    packed = built.reshape(row_count, slot_count * group_count * HEAD_SIZE)
+    key_piece = ctx_gather(rows_of_keys, 0, True)
+    value_piece = ctx_gather(packed, 0, True)
     piece_rows = key_piece.shape[0]
     step_rows = block_rows(piece_rows)
 
@@ -133,8 +167,7 @@
         offset = block_index * step_rows
         key_block = lax.dynamic_slice_in_dim(key_piece, offset, step_rows, 0)
         value_block = lax.dynamic_slice_in_dim(value_piece, offset, step_rows, 0)
-        key_start = first_row + offset
-        return update(current, key_block, value_block, key_start)
+        return update(current, key_block, value_block, offset)
 
     run_max, run_total, accumulated = lax.fori_loop(0, piece_rows // step_rows, advance, initial)
     result = accumulated / run_total[..., None]

time: 112 us -> 75 us (0.67)
  blocking collectives: 70.8 us -> 0 us
  starting transfers between devices: 0.09 us -> 22.6 us
  waiting for transfers between devices: 9.9 us -> 23.1 us
  matrix products: 13.1 us -> 2.68 us
  other arithmetic: 1.96 us -> 10.2 us
  between operations: 14 us -> 10.4 us
  local copies, waits for them, and re-layouts: 1.87 us -> 5.36 us
    all_gather x7 -> x0, blocking collectives: 49.6 us -> none  [the longest x1 12 us: per_device(): lax.all_gather(value_down, 'ctx', axis=1, tiled=True)]
    ppermute x0 -> x19, waiting for transfers between devices: none -> 23.1 us  [swap(): return lax.ppermute(value, axis, [(i, i ^ bit) for i in range(size)])]
    ppermute x0 -> x19, starting transfers between devices: none -> 22.6 us  [swap(): return lax.ppermute(value, axis, [(i, i ^ bit) for i in range(size)])]
    psum x1 -> x0, blocking collectives: 21.2 us -> none  [per_device(): rank_query, rank_value = lax.psum((rank_query, rank_value), 'mp')]
    all_gather x3 -> x0, waiting for transfers between devices: 9.85 us -> none  [the longest x1 9.81 us: per_device(): lax.all_gather(full_rank[0], 'req', axis=0, tiled=True)]
    dot_general x5 -> x1, matrix products: 9.93 us -> 0.24 us  [per_device(): jnp.einsum('rsk,skc->rsc', rank_value, up_value, preferred_element_type=j...]
    select_n x0 -> x9, other arithmetic: none -> 5.94 us  [the longest x4 2.95 us: select_members(): slots.append(jnp.where(m // row_span == row, near, received[s]))]
    slice x0 -> x2, local copies, waits for them, and re-layouts: none -> 1.99 us  [the longest x1 1.39 us: select_members(): m = member_ids[s]]
  transfers between devices with their start and end apart: 3 -> 19, of which waited for: 1 -> 6; matrix products, arithmetic and copies ran while one was open for 7% -> 22% of each run, Pallas kernels for 0% -> 0%
where the time goes in v1:
time: 75 us; the launch traced here: 74.3 us
  waiting for transfers between devices  23.1 us (31%)
  starting transfers between devices  22.6 us (30%)
  between operations  10.4 us (14%)
  other arithmetic  10.2 us (14%)
  local copies, waits for them, and re-layouts  5.36 us (7%)
  matrix products  2.68 us (4%)
    ppermute x19, waiting for transfers between devices, swap(): return lax.ppermute(value, axis, [(i, i ^ bit) for i in range(size)])  23.1 us
    ppermute x19, starting transfers between devices, swap(): return lax.ppermute(value, axis, [(i, i ^ bit) for i in range(size)])  22.6 us
    select_n x4, other arithmetic, select_members(): slots.append(jnp.where(m // row_span == row, near, received[s]))  2.95 us
    select_n x3, other arithmetic, pick(): return jnp.where(index // local_count == core, mine, theirs)  2.11 us
  transfers between devices with their start and end apart: 19, of which 6 were waited for; matrix products, arithmetic and copies ran while one was open for 22% of the time, Pallas kernels for 0%

profile of v1, /device:TPU:0, one launch (start us, length us, event | category | flops | bytes accessed | tf_op | source)
XLA Modules:
  0.0 74.3 jit_solution(10833791296399485594)
XLA Ops:
  0.0 3.1 %collective-permute-start.2 = (s32[1,2]{1,0:T(1,128)}, s32[1,2]{1,0:T(1,128)S(1)}, u32[]{:S(2)}, u32[]{:S(2)}) collective-permute-start(s32[1,2]{1,0:T(1,128)} %param.18), channel_id=1, source_target_pairs={{0,8},{4,12},{8,0},{12,4},{1,9},{5,13},{9,1},{13,5},{2,10},{6,14},... | collective-permute-start | bytes 32 | tf_op jit(solution)/shard_map/ppermute | solution.py:22
  3.1 0.9 %copy.18 = bf16[1,128,256]{1,2,0:T(8,128)(2,1)S(1)} copy(bf16[1,128,256]{2,1,0:T(8,128)(2,1)} %param.12) | data formatting | bytes 131072 | tf_op args[2]
  4.0 1.6 %collective-permute-start = (bf16[128,256]{0,1:T(8,128)(2,1)S(1)}, bf16[128,256]{0,1:T(8,128)(2,1)}, u32[]{:S(2)}, u32[]{:S(2)}) collective-permute-start(bf16[128,256]{0,1:T(8,128)(2,1)S(1)} %bitcast.81), channel_id=1, source_target_pairs={{0,16},{16,0},{1,17},{17,1},{2,18},{18,2},{3,19},{19,3},{4,20},{20... | collective-permute-start | bytes 196616 | tf_op jit(solution)/shard_map/ppermute | solution.py:22
  5.6 0.2 collective-permute-start.5
  5.8 0.3 collective-permute-start.1
  6.8 0.9 %bitcast_convert_fusion.1 = f32[128,256]{1,0:T(8,128)S(1)} fusion(bf16[1,128,256]{2,1,0:T(8,128)(2,1)} %param.13), kind=kLoop, calls=%fused_computation.67 | loop fusion | flops 32768 | bytes 196608 | tf_op jit(solution)/shard_map/convert_element_type | solution.py:157
  7.6 1.1 %bitcast_convert_fusion = f32[128,2048]{1,0:T(8,128)S(1)} fusion(bf16[1,128,2048]{2,1,0:T(8,128)(2,1)} %param.11), kind=kLoop, calls=%fused_computation.35 | loop fusion | flops 262144 | bytes 1572864 | tf_op jit(solution)/shard_map/convert_element_type | solution.py:110
  8.8 0.1 fusion.32
  8.9 0.3 collective-permute-start.13
  9.2 0.6 fusion.43
  13.8 0.8 %dynamic-slice_select_fusion.7 = (bf16[1,32,256]{2,1,0:T(8,128)(2,1)S(1)}, bf16[1,32,256]{2,1,0:T(8,128)(2,1)S(1)}) fusion(bf16[2,32,256]{2,1,0:T(8,128)(2,1)S(1)} %collective-permute-done.10, s32[]{:T(128)S(6)} %select_n.402, bf16[2,32,256]{2,1,0:T(8,128)(2,1)} %param.17, pred[]{:T(512)S(6)} %eq.93, s32[]{:T(128)S(6)} %select_n.408, pred[]{:T(512)S(6)} %eq.94), kind=kLoop, calls=%fused_computation.78 | loop fusion | flops 16384 | bytes 98314 | tf_op jit(solution)/shard_map/jit(_where)/select_n | solution.py:67
  14.6 0.6 pad_maximum_fusion.8
  15.2 0.5 collective-permute-start.11
  15.7 1.4 %fusion.42 = (s32[1,1]{1,0:T(1,128)}, s32[1,1]{1,0:T(1,128)}) fusion(s32[1,2]{1,0:T(1,128)} %param.18), kind=kLoop, calls=%fused_computation.87 | loop fusion | bytes 16 | tf_op jit(solution)/shard_map/slice | solution.py:78
  22.6 0.8 %copy.23 = f32[128,256]{0,1:T(8,128)} copy(f32[128,256]{1,0:T(8,128)S(1)} %bitcast_convert_fusion.1) | data formatting | bytes 262144 | tf_op jit(solution)/shard_map/convert_element_type | solution.py:157
  23.3 0.3 copy.19
  23.7 0.8 %slice_select_fusion.7 = (bf16[1,32,256]{2,1,0:T(8,128)(2,1)S(1)}, bf16[1,32,256]{2,1,0:T(8,128)(2,1)S(1)}) fusion(bf16[2,32,256]{2,1,0:T(8,128)(2,1)} %collective-permute-done.11, bf16[2,32,256]{2,1,0:T(8,128)(2,1)} %copy-done.6, s32[]{:T(128)S(6)} %select_n.396, bf16[2,32,256]{2,1,0:T(8,128)(2,1)S(1)} %copy-done.5, pred[]{:T(512)S(6)} %eq.92, pred[]{:T(512)S(6)} %eq.91, ...), kind=kLoop, calls=%fused_computation.75 | loop fusion | flops 32768 | bytes 131084 | tf_op jit(solution)/shard_map/jit(_where)/select_n | solution.py:80
  24.5 0.4 collective-permute-start.12
  25.0 0.9 %broadcast_select_fusion.3 = (bf16[128,256]{0,1:T(8,128)(2,1)S(1)}, bf16[128,256]{0,1:T(8,128)(2,1)S(1)}) fusion(bf16[128,256]{0,1:T(8,128)(2,1)} %collective-permute-done, pred[]{:T(512)S(6)} %eq.90, bf16[1,128,256]{1,2,0:T(8,128)(2,1)S(1)} %copy.18), kind=kLoop, calls=%fused_computation.71 | loop fusion | flops 65536 | bytes 262145 | tf_op jit(solution)/shard_map/jit(_where)/select_n | solution.py:31
  25.9 1.3 %dynamic-slice_select_fusion.1 = (bf16[1,32,2048]{2,1,0:T(8,128)(2,1)S(1)}, bf16[1,32,2048]{2,1,0:T(8,128)(2,1)S(1)}, bf16[1,32,2048]{2,1,0:T(8,128)(2,1)S(1)}, bf16[1,32,2048]{2,1,0:T(8,128)(2,1)S(1)}) fusion(bf16[2,32,2048]{2,1,0:T(8,128)(2,1)} %collective-permute-done.13, s32[]{:T(128)S(6)} %select_n.402, bf16[2,32,2048]{2,1,0:T(8,128)(2,1)} %param.16, ...), kind=kLoop, calls=%fused_computation.53 | loop fusion | flops 262144 | bytes 1572874 | tf_op jit(solution)/shard_map/jit(_where)/select_n | solution.py:67
  27.2 1.8 %collective-permute-start.6 = (bf16[2,32,2048]{2,1,0:T(8,128)(2,1)S(1)}, bf16[2,32,2048]{2,1,0:T(8,128)(2,1)S(1)}, u32[]{:S(2)}, u32[]{:S(2)}) collective-permute-start(bf16[2,32,2048]{2,1,0:T(8,128)(2,1)S(1)} %pad_maximum_fusion.2), channel_id=1, source_target_pairs={{0,8},{4,12},{8,0},{12,4},{1,9},{5,13},{9,1},{13,5},{2,10},{6,14},... | collective-permute-start | bytes 786440 | tf_op jit(solution)/shard_map/ppermute | solution.py:22
  29.0 0.4 collective-permute-start.3
  29.4 1.8 %collective-permute-start.14 = (bf16[2,32,2048]{2,1,0:T(8,128)(2,1)S(1)}, bf16[2,32,2048]{2,1,0:T(8,128)(2,1)S(1)}, u32[]{:S(2)}, u32[]{:S(2)}) collective-permute-start(bf16[2,32,2048]{2,1,0:T(8,128)(2,1)S(1)} %pad_maximum_fusion.4), channel_id=1, source_target_pairs={{0,8},{4,12},{8,0},{12,4},{1,9},{5,13},{9,1},{13,5},{2,10},{6,14},... | collective-permute-start | bytes 786440 | tf_op jit(solution)/shard_map/ppermute | solution.py:22
  31.2 5.2 %collective-permute-done.6 = bf16[2,32,2048]{2,1,0:T(8,128)(2,1)S(1)} collective-permute-done((bf16[2,32,2048]{2,1,0:T(8,128)(2,1)S(1)}, bf16[2,32,2048]{2,1,0:T(8,128)(2,1)S(1)}, u32[]{:S(2)}, u32[]{:S(2)}) %collective-permute-start.6) | collective-permute-done | bytes 262176 | tf_op jit(solution)/shard_map/ppermute | solution.py:22
  36.4 1.0 %slice_select_fusion.3 = (bf16[1,32,2048]{2,1,0:T(8,128)(2,1)S(1)}, bf16[1,32,2048]{2,1,0:T(8,128)(2,1)S(1)}) fusion(bf16[2,32,2048]{2,1,0:T(8,128)(2,1)S(1)} %collective-permute-done.6, bf16[2,32,2048]{2,1,0:T(8,128)(2,1)} %collective-permute-done.5, s32[]{:T(128)S(6)} %select_n.396, bf16[2,32,2048]{2,1,0:T(8,128)(2,1)S(1)} %copy-done.2, pred[]{:T(512)S(6)} %eq.92, ...), kind=kLoop, calls=%fused_computation.48 | loop fusion | flops 262144 | bytes 1048588 | tf_op jit(solution)/shard_map/jit(_where)/select_n | solution.py:80
  37.5 1.7 %collective-permute-start.7 = (bf16[2,32,2048]{2,1,0:T(8,128)(2,1)S(1)}, bf16[2,32,2048]{2,1,0:T(8,128)(2,1)S(1)}, u32[]{:S(2)}, u32[]{:S(2)}) collective-permute-start(bf16[2,32,2048]{2,1,0:T(8,128)(2,1)S(1)} %pad_maximum_fusion.3), channel_id=1, source_target_pairs={{0,16},{16,0},{1,17},{17,1},{2,18},{18,2},{3,19},{19,3},{4,20},{20... | collective-permute-start | bytes 786440 | tf_op jit(solution)/shard_map/ppermute | solution.py:22
  39.2 7.1 %collective-permute-done.14 = bf16[2,32,2048]{2,1,0:T(8,128)(2,1)S(1)} collective-permute-done((bf16[2,32,2048]{2,1,0:T(8,128)(2,1)S(1)}, bf16[2,32,2048]{2,1,0:T(8,128)(2,1)S(1)}, u32[]{:S(2)}, u32[]{:S(2)}) %collective-permute-start.14) | collective-permute-done | bytes 262176 | tf_op jit(solution)/shard_map/ppermute | solution.py:22
  46.3 1.0 %slice_select_fusion.1 = (bf16[1,32,2048]{2,1,0:T(8,128)(2,1)S(1)}, bf16[1,32,2048]{2,1,0:T(8,128)(2,1)S(1)}) fusion(bf16[2,32,2048]{2,1,0:T(8,128)(2,1)S(1)} %collective-permute-done.14, bf16[2,32,2048]{2,1,0:T(8,128)(2,1)} %collective-permute-done.13, s32[]{:T(128)S(6)} %select_n.396, bf16[2,32,2048]{2,1,0:T(8,128)(2,1)S(1)} %copy-done.3, pred[]{:T(512)S(6)} %eq.92, ...), kind=kLoop, calls=%fused_computation.46 | loop fusion | flops 262144 | bytes 1048588 | tf_op jit(solution)/shard_map/jit(_where)/select_n | solution.py:80
  47.4 1.8 %collective-permute-start.15 = (bf16[2,32,2048]{2,1,0:T(8,128)(2,1)S(1)}, bf16[2,32,2048]{2,1,0:T(8,128)(2,1)S(1)}, u32[]{:S(2)}, u32[]{:S(2)}) collective-permute-start(bf16[2,32,2048]{2,1,0:T(8,128)(2,1)S(1)} %pad_maximum_fusion.5), channel_id=1, source_target_pairs={{0,16},{16,0},{1,17},{17,1},{2,18},{18,2},{3,19},{19,3},{4,20},{20... | collective-permute-start | bytes 786440 | tf_op jit(solution)/shard_map/ppermute | solution.py:22
  49.2 0.1 slice_select_fusion.5
  49.3 0.4 collective-permute-start.4
  49.6 7.0 %collective-permute-done.15 = bf16[2,32,2048]{2,1,0:T(8,128)(2,1)S(1)} collective-permute-done((bf16[2,32,2048]{2,1,0:T(8,128)(2,1)S(1)}, bf16[2,32,2048]{2,1,0:T(8,128)(2,1)S(1)}, u32[]{:S(2)}, u32[]{:S(2)}) %collective-permute-start.15) | collective-permute-done | bytes 262176 | tf_op jit(solution)/shard_map/ppermute | solution.py:22
  56.6 0.3 convolution_bitcast_fusion.2
  57.0 1.9 %collective-permute-start.16 = (f32[128,2,64]{0,2,1:T(8,128)S(1)}, f32[128,2,64]{0,2,1:T(8,128)S(1)}, u32[]{:S(2)}, u32[]{:S(2)}) collective-permute-start(f32[128,2,64]{0,2,1:T(8,128)S(1)} %convolution_bitcast_fusion.2), channel_id=1, source_target_pairs={{0,1},{1,0},{2,3},{3,2},{4,5},{5,4},{6,7},{7,6},{8,9},{9,8},{10,11... | collective-permute-start | bytes 196616 | tf_op jit(solution)/shard_map/ppermute | solution.py:22
  58.8 0.3 convolution_bitcast_fusion.3
  59.1 0.3 collective-permute-start.8
  59.4 1.9 %collective-permute-done.16 = f32[128,2,64]{0,2,1:T(8,128)S(1)} collective-permute-done((f32[128,2,64]{0,2,1:T(8,128)S(1)}, f32[128,2,64]{0,2,1:T(8,128)S(1)}, u32[]{:S(2)}, u32[]{:S(2)}) %collective-permute-start.16) | collective-permute-done | bytes 65568 | tf_op jit(solution)/shard_map/ppermute | solution.py:22
  61.4 3.1 %collective-permute-start.17 = (f32[128,2,64]{0,2,1:T(8,128)S(1)}, f32[128,2,64]{0,2,1:T(8,128)S(1)}, u32[]{:S(2)}, u32[]{:S(2)}) collective-permute-start(f32[128,2,64]{0,2,1:T(8,128)S(1)} %add.200), channel_id=1, source_target_pairs={{0,2},{1,3},{2,0},{3,1},{4,6},{5,7},{6,4},{7,5},{8,10},{9,11},{10,... | collective-permute-start | bytes 196616 | tf_op jit(solution)/shard_map/ppermute | solution.py:22
  64.5 1.6 %collective-permute-start.9 = (f32[128,2,64]{0,2,1:T(8,128)S(1)}, f32[128,2,64]{0,2,1:T(8,128)S(1)}, u32[]{:S(2)}, u32[]{:S(2)}) collective-permute-start(f32[128,2,64]{0,2,1:T(8,128)S(1)} %add.196), channel_id=1, source_target_pairs={{0,2},{1,3},{2,0},{3,1},{4,6},{5,7},{6,4},{7,5},{8,10},{9,11},{10,... | collective-permute-start | bytes 196616 | tf_op jit(solution)/shard_map/ppermute | solution.py:22
  66.1 0.6 collective-permute-done.17
  66.7 0.2 fusion.12
  67.0 1.6 %collective-permute-start.18 = (bf16[128,512]{0,1:T(8,128)(2,1)S(1)}, bf16[128,512]{0,1:T(8,128)(2,1)S(1)}, u32[]{:S(2)}, u32[]{:S(2)}) collective-permute-start(bf16[128,512]{0,1:T(8,128)(2,1)S(1)} %bitcast.78), channel_id=1, source_target_pairs={{0,16},{16,0},{1,17},{17,1},{2,18},{18,2},{3,19},{19,3},{4,20},{20... | collective-permute-start | bytes 393224 | tf_op jit(solution)/shard_map/ppermute | solution.py:22
  68.6 1.2 %collective-permute-done.9 = f32[128,2,64]{0,2,1:T(8,128)S(1)} collective-permute-done((f32[128,2,64]{0,2,1:T(8,128)S(1)}, f32[128,2,64]{0,2,1:T(8,128)S(1)}, u32[]{:S(2)}, u32[]{:S(2)}) %collective-permute-start.9) | collective-permute-done | bytes 65568 | tf_op jit(solution)/shard_map/ppermute | solution.py:22
  69.8 0.5 fusion.4
  70.3 0.8 %fusion = (f32[2,2,8,128]{3,2,0,1:T(8,128)S(1)}, f32[2,256,128,2,8]{2,1,4,3,0:T(8,128)S(1)}) fusion(pred[128,256]{0,1:T(8,128)(4,1)S(1)} %fusion.32, bf16[256,2,128,1,1]{0,2,4,3,1:T(8,128)(2,1)S(1)} %bitcast.79, bf16[128,2,2,8,128]{0,4,3,2,1:T(8,128)(2,1)S(1)} %bitcast.76), kind=kOutput, calls=%fused_computation.2 | convolution fusion | flops 271577088 | bytes 5423104 | tf_op jit(solution)/shard_map/while/body/eval_jaxpr/rsgjd,kgd->sgjrk/dot_general | solution.py:128
  71.1 1.3 %fusion.1 = (f32[2,2,8,128]{3,2,0,1:T(8,128)S(1)}, bf16[2,2,8,128,256]{3,4,2,0,1:T(8,128)(2,1)S(1)}) fusion(f32[2,256,128,2,8]{2,1,4,3,0:T(8,128)S(1)} %get-tuple-element.64, f32[2,2,8,128]{3,2,0,1:T(8,128)S(1)} %get-tuple-element.58, pred[128,256]{0,1:T(8,128)(4,1)S(1)} %fusion.32), kind=kLoop, calls=%fused_computation.3 | loop fusion | flops 6287360 | bytes 6356992 | tf_op jit(solution)/shard_map/while/body/eval_jaxpr/reduce_sum | solution.py:141
  72.5 0.5 fusion.6
  73.0 1.3 %copy.26 = bf16[2,1,128,2048]{3,2,1,0:T(8,128)(2,1)} copy(bf16[2,1,128,2048]{2,3,0,1:T(8,128)(2,1)S(1)} %bitcast.77) | data formatting | bytes 2097152 | tf_op jit(solution)/shard_map/convert_element_type | solution.py:177
  (45 shorter events, 0.4 us)
Async XLA Ops:
  0.0 56.6 %copy-start = (bf16[1,128,2048]{2,1,0:T(8,128)(2,1)S(1)}, bf16[1,128,2048]{2,1,0:T(8,128)(2,1)}, u32[]{:S(2)}) copy-start(bf16[1,128,2048]{2,1,0:T(8,128)(2,1)} %param.10) | copy-start | bytes 1572868
  0.0 23.7 %copy-start.5 = (bf16[2,32,256]{2,1,0:T(8,128)(2,1)S(1)}, bf16[2,32,256]{2,1,0:T(8,128)(2,1)}, u32[]{:S(2)}) copy-start(bf16[2,32,256]{2,1,0:T(8,128)(2,1)} %param.17) | copy-start | bytes 98308
  0.0 25.8 %copy-start.2 = (bf16[2,32,2048]{2,1,0:T(8,128)(2,1)S(1)}, bf16[2,32,2048]{2,1,0:T(8,128)(2,1)}, u32[]{:S(2)}) copy-start(bf16[2,32,2048]{2,1,0:T(8,128)(2,1)} %param.14) | copy-start | bytes 786436
  0.0 28.9 %copy-start.1 = (bf16[2,32,2048]{2,1,0:T(8,128)(2,1)S(1)}, bf16[2,32,2048]{2,1,0:T(8,128)(2,1)}, u32[]{:S(2)}) copy-start(bf16[2,32,2048]{2,1,0:T(8,128)(2,1)} %param.15) | copy-start | bytes 786436
  0.0 8.9 %collective-permute-start.2 = (s32[1,2]{1,0:T(1,128)}, s32[1,2]{1,0:T(1,128)S(1)}, u32[]{:S(2)}, u32[]{:S(2)}) collective-permute-start(s32[1,2]{1,0:T(1,128)} %param.18), channel_id=1, source_target_pairs={{0,8},{4,12},{8,0},{12,4},{1,9},{5,13},{9,1},{13,5},{2,10},{6,14},... | collective-permute-start | bytes 32 | tf_op jit(solution)/shard_map/ppermute | solution.py:22
  3.1 10.7 %collective-permute-start.10 = (bf16[2,32,256]{2,1,0:T(8,128)(2,1)}, bf16[2,32,256]{2,1,0:T(8,128)(2,1)S(1)}, u32[]{:S(2)}, u32[]{:S(2)}) collective-permute-start(bf16[2,32,256]{2,1,0:T(8,128)(2,1)} %param.17), channel_id=1, source_target_pairs={{0,4},{4,0},{8,12},{12,8},{1,5},{5,1},{9,13},{13,9},{2,6},{6,2},{1... | collective-permute-start | bytes 98312 | tf_op jit(solution)/shard_map/ppermute | solution.py:22
  4.0 20.9 %collective-permute-start = (bf16[128,256]{0,1:T(8,128)(2,1)S(1)}, bf16[128,256]{0,1:T(8,128)(2,1)}, u32[]{:S(2)}, u32[]{:S(2)}) collective-permute-start(bf16[128,256]{0,1:T(8,128)(2,1)S(1)} %bitcast.81), channel_id=1, source_target_pairs={{0,16},{16,0},{1,17},{17,1},{2,18},{18,2},{3,19},{19,3},{4,20},{20... | collective-permute-start | bytes 196616 | tf_op jit(solution)/shard_map/ppermute | solution.py:22
  5.6 20.2 %collective-permute-start.5 = (bf16[2,32,2048]{2,1,0:T(8,128)(2,1)}, bf16[2,32,2048]{2,1,0:T(8,128)(2,1)}, u32[]{:S(2)}, u32[]{:S(2)}) collective-permute-start(bf16[2,32,2048]{2,1,0:T(8,128)(2,1)} %param.14), channel_id=1, source_target_pairs={{0,4},{4,0},{8,12},{12,8},{1,5},{5,1},{9,13},{13,9},{2,6},{6,2},{1... | collective-permute-start | bytes 786440 | tf_op jit(solution)/shard_map/ppermute | solution.py:22
  5.8 23.1 %collective-permute-start.1 = (bf16[2,32,2048]{2,1,0:T(8,128)(2,1)}, bf16[2,32,2048]{2,1,0:T(8,128)(2,1)S(1)}, u32[]{:S(2)}, u32[]{:S(2)}) collective-permute-start(bf16[2,32,2048]{2,1,0:T(8,128)(2,1)} %param.15), channel_id=1, source_target_pairs={{0,4},{4,0},{8,12},{12,8},{1,5},{5,1},{9,13},{13,9},{2,6},{6,2},{1... | collective-permute-start | bytes 786440 | tf_op jit(solution)/shard_map/ppermute | solution.py:22
  8.9 16.9 %collective-permute-start.13 = (bf16[2,32,2048]{2,1,0:T(8,128)(2,1)}, bf16[2,32,2048]{2,1,0:T(8,128)(2,1)}, u32[]{:S(2)}, u32[]{:S(2)}) collective-permute-start(bf16[2,32,2048]{2,1,0:T(8,128)(2,1)} %param.16), channel_id=1, source_target_pairs={{0,4},{4,0},{8,12},{12,8},{1,5},{5,1},{9,13},{13,9},{2,6},{6,2},{1... | collective-permute-start | bytes 786440 | tf_op jit(solution)/shard_map/ppermute | solution.py:22
  13.8 8.8 %copy-start.6 = (bf16[2,32,256]{2,1,0:T(8,128)(2,1)}, bf16[2,32,256]{2,1,0:T(8,128)(2,1)S(1)}, u32[]{:S(2)}) copy-start(bf16[2,32,256]{2,1,0:T(8,128)(2,1)S(1)} %collective-permute-done.10) | copy-start | bytes 98308
  15.2 8.5 %collective-permute-start.11 = (bf16[2,32,256]{2,1,0:T(8,128)(2,1)}, bf16[2,32,256]{2,1,0:T(8,128)(2,1)}, u32[]{:S(2)}, u32[]{:S(2)}) collective-permute-start(bf16[2,32,256]{2,1,0:T(8,128)(2,1)} %pad_maximum_fusion.8), channel_id=1, source_target_pairs={{0,8},{4,12},{8,0},{12,4},{1,9},{5,13},{9,1},{13,5},{2,10},{6,14},... | collective-permute-start | bytes 98312 | tf_op jit(solution)/shard_map/ppermute | solution.py:22
  23.7 22.6 %copy-start.3 = (bf16[2,32,2048]{2,1,0:T(8,128)(2,1)S(1)}, bf16[2,32,2048]{2,1,0:T(8,128)(2,1)}, u32[]{:S(2)}) copy-start(bf16[2,32,2048]{2,1,0:T(8,128)(2,1)} %param.16) | copy-start | bytes 786436
  24.5 41.6 %collective-permute-start.12 = (bf16[2,32,256]{2,1,0:T(8,128)(2,1)S(1)}, bf16[2,32,256]{2,1,0:T(8,128)(2,1)S(1)}, u32[]{:S(2)}, u32[]{:S(2)}) collective-permute-start(bf16[2,32,256]{2,1,0:T(8,128)(2,1)S(1)} %pad_maximum_fusion.9), channel_id=1, source_target_pairs={{0,16},{16,0},{1,17},{17,1},{2,18},{18,2},{3,19},{19,3},{4,20},{20... | collective-permute-start | bytes 98312 | tf_op jit(solution)/shard_map/ppermute | solution.py:22
  27.2 9.2 %collective-permute-start.6 = (bf16[2,32,2048]{2,1,0:T(8,128)(2,1)S(1)}, bf16[2,32,2048]{2,1,0:T(8,128)(2,1)S(1)}, u32[]{:S(2)}, u32[]{:S(2)}) collective-permute-start(bf16[2,32,2048]{2,1,0:T(8,128)(2,1)S(1)} %pad_maximum_fusion.2), channel_id=1, source_target_pairs={{0,8},{4,12},{8,0},{12,4},{1,9},{5,13},{9,1},{13,5},{2,10},{6,14},... | collective-permute-start | bytes 786440 | tf_op jit(solution)/shard_map/ppermute | solution.py:22
  29.0 20.2 %collective-permute-start.3 = (bf16[2,32,2048]{2,1,0:T(8,128)(2,1)S(1)}, bf16[2,32,2048]{2,1,0:T(8,128)(2,1)S(1)}, u32[]{:S(2)}, u32[]{:S(2)}) collective-permute-start(bf16[2,32,2048]{2,1,0:T(8,128)(2,1)S(1)} %pad_maximum_fusion), channel_id=1, source_target_pairs={{0,8},{4,12},{8,0},{12,4},{1,9},{5,13},{9,1},{13,5},{2,10},{6,14},... | collective-permute-start | bytes 786440 | tf_op jit(solution)/shard_map/ppermute | solution.py:22
  29.4 16.9 %collective-permute-start.14 = (bf16[2,32,2048]{2,1,0:T(8,128)(2,1)S(1)}, bf16[2,32,2048]{2,1,0:T(8,128)(2,1)S(1)}, u32[]{:S(2)}, u32[]{:S(2)}) collective-permute-start(bf16[2,32,2048]{2,1,0:T(8,128)(2,1)S(1)} %pad_maximum_fusion.4), channel_id=1, source_target_pairs={{0,8},{4,12},{8,0},{12,4},{1,9},{5,13},{9,1},{13,5},{2,10},{6,14},... | collective-permute-start | bytes 786440 | tf_op jit(solution)/shard_map/ppermute | solution.py:22
  37.4 29.3 %copy-start.4 = (f32[128,256]{0,1:T(8,128)S(1)}, f32[128,256]{0,1:T(8,128)}, u32[]{:S(2)}) copy-start(f32[128,256]{0,1:T(8,128)} %copy.23) | copy-start | bytes 393220
  37.5 21.3 %collective-permute-start.7 = (bf16[2,32,2048]{2,1,0:T(8,128)(2,1)S(1)}, bf16[2,32,2048]{2,1,0:T(8,128)(2,1)S(1)}, u32[]{:S(2)}, u32[]{:S(2)}) collective-permute-start(bf16[2,32,2048]{2,1,0:T(8,128)(2,1)S(1)} %pad_maximum_fusion.3), channel_id=1, source_target_pairs={{0,16},{16,0},{1,17},{17,1},{2,18},{18,2},{3,19},{19,3},{4,20},{20... | collective-permute-start | bytes 786440 | tf_op jit(solution)/shard_map/ppermute | solution.py:22
  47.4 9.2 %collective-permute-start.15 = (bf16[2,32,2048]{2,1,0:T(8,128)(2,1)S(1)}, bf16[2,32,2048]{2,1,0:T(8,128)(2,1)S(1)}, u32[]{:S(2)}, u32[]{:S(2)}) collective-permute-start(bf16[2,32,2048]{2,1,0:T(8,128)(2,1)S(1)} %pad_maximum_fusion.5), channel_id=1, source_target_pairs={{0,16},{16,0},{1,17},{17,1},{2,18},{18,2},{3,19},{19,3},{4,20},{20... | collective-permute-start | bytes 786440 | tf_op jit(solution)/shard_map/ppermute | solution.py:22
  49.3 19.3 %collective-permute-start.4 = (bf16[2,32,2048]{2,1,0:T(8,128)(2,1)S(1)}, bf16[2,32,2048]{2,1,0:T(8,128)(2,1)S(1)}, u32[]{:S(2)}, u32[]{:S(2)}) collective-permute-start(bf16[2,32,2048]{2,1,0:T(8,128)(2,1)S(1)} %pad_maximum_fusion.1), channel_id=1, source_target_pairs={{0,16},{16,0},{1,17},{17,1},{2,18},{18,2},{3,19},{19,3},{4,20},{20... | collective-permute-start | bytes 786440 | tf_op jit(solution)/shard_map/ppermute | solution.py:22
  57.0 4.4 %collective-permute-start.16 = (f32[128,2,64]{0,2,1:T(8,128)S(1)}, f32[128,2,64]{0,2,1:T(8,128)S(1)}, u32[]{:S(2)}, u32[]{:S(2)}) collective-permute-start(f32[128,2,64]{0,2,1:T(8,128)S(1)} %convolution_bitcast_fusion.2), channel_id=1, source_target_pairs={{0,1},{1,0},{2,3},{3,2},{4,5},{5,4},{6,7},{7,6},{8,9},{9,8},{10,11... | collective-permute-start | bytes 196616 | tf_op jit(solution)/shard_map/ppermute | solution.py:22
  59.1 5.4 %collective-permute-start.8 = (f32[128,2,64]{0,2,1:T(8,128)S(1)}, f32[128,2,64]{0,2,1:T(8,128)S(1)}, u32[]{:S(2)}, u32[]{:S(2)}) collective-permute-start(f32[128,2,64]{0,2,1:T(8,128)S(1)} %convolution_bitcast_fusion.3), channel_id=1, source_target_pairs={{0,1},{1,0},{2,3},{3,2},{4,5},{5,4},{6,7},{7,6},{8,9},{9,8},{10,11... | collective-permute-start | bytes 196616 | tf_op jit(solution)/shard_map/ppermute | solution.py:22
  61.4 5.4 %collective-permute-start.17 = (f32[128,2,64]{0,2,1:T(8,128)S(1)}, f32[128,2,64]{0,2,1:T(8,128)S(1)}, u32[]{:S(2)}, u32[]{:S(2)}) collective-permute-start(f32[128,2,64]{0,2,1:T(8,128)S(1)} %add.200), channel_id=1, source_target_pairs={{0,2},{1,3},{2,0},{3,1},{4,6},{5,7},{6,4},{7,5},{8,10},{9,11},{10,... | collective-permute-start | bytes 196616 | tf_op jit(solution)/shard_map/ppermute | solution.py:22
  64.5 5.2 %collective-permute-start.9 = (f32[128,2,64]{0,2,1:T(8,128)S(1)}, f32[128,2,64]{0,2,1:T(8,128)S(1)}, u32[]{:S(2)}, u32[]{:S(2)}) collective-permute-start(f32[128,2,64]{0,2,1:T(8,128)S(1)} %add.196), channel_id=1, source_target_pairs={{0,2},{1,3},{2,0},{3,1},{4,6},{5,7},{6,4},{7,5},{8,10},{9,11},{10,... | collective-permute-start | bytes 196616 | tf_op jit(solution)/shard_map/ppermute | solution.py:22
  67.0 5.4 %collective-permute-start.18 = (bf16[128,512]{0,1:T(8,128)(2,1)S(1)}, bf16[128,512]{0,1:T(8,128)(2,1)S(1)}, u32[]{:S(2)}, u32[]{:S(2)}) collective-permute-start(bf16[128,512]{0,1:T(8,128)(2,1)S(1)} %bitcast.78), channel_id=1, source_target_pairs={{0,16},{16,0},{1,17},{17,1},{2,18},{18,2},{3,19},{19,3},{4,20},{20... | collective-permute-start | bytes 393224 | tf_op jit(solution)/shard_map/ppermute | solution.py:22

commit v2 on v1

--- a/solution.py
+++ b/solution.py
@@ -34,15 +34,14 @@
     return lax.all_gather(mine, "ctx", axis=dim, tiled=True)
 
 
-def mp_sum(values):
+def mp_sum(value):
     size = lax.axis_size("mp")
     if size & (size - 1):
-        return lax.psum(values, "mp")
-    bit = 1
-    while bit < size:
-        values = jax.tree.map(lambda a, b: a + b, values, swap(values, "mp", bit))
-        bit *= 2
-    return values
+        return lax.psum(value, "mp")
+    total = value
+    for bit in range(1, size):
+        total = total + swap(value, "mp", bit)
+    return total
 
 
 def select_members(factor_set, member_ids, member_lists):
@@ -96,16 +95,20 @@
 ):
     row_count = activations.shape[1]
     member_ids = member_lists[0]
-    halves = select_members(
-        (query_down, value_down, query_up, value_raise_factor), member_ids, member_lists
-    )
-    down_query, down_value, up_query, up_value = [ctx_gather(h, 1, False) for h in halves]
+    local_count, rank_part, width = query_down.shape
+    up_width = query_up.shape[2]
+    downs = jnp.stack([query_down, value_down], axis=1)
+    ups = jnp.concatenate([query_up, value_raise_factor], axis=2)
+    down_half, up_half = select_members((downs, ups), member_ids, member_lists)
+    downs = ctx_gather(down_half, 2, False)
+    ups = ctx_gather(up_half, 1, False)
     tokens = activations[0]
-    rank_query = jnp.einsum("rd,skd->rsk", tokens, down_query, preferred_element_type=jnp.float32)
-    rank_value = jnp.einsum("rd,skd->rsk", tokens, down_value, preferred_element_type=jnp.float32)
-    rank_query, rank_value = mp_sum((rank_query, rank_value))
-    rank_query = rank_query.astype(jnp.bfloat16)
-    rank_value = rank_value.astype(jnp.bfloat16)
+    ranks = jnp.einsum("rd,sfkd->rfsk", tokens, downs, preferred_element_type=jnp.float32)
+    ranks = mp_sum(ranks).astype(jnp.bfloat16)
+    rank_query = ranks[:, 0]
+    rank_value = ranks[:, 1]
+    up_query = ups[..., :up_width]
+    up_value = ups[..., up_width:]
     query_matrix = (
         query_base[0][:, None, :]
         + jnp.einsum("rsk,skc->rsc", rank_query, up_query, preferred_element_type=jnp.float32)

time: 75 us -> 74.6 us (level)
  starting transfers between devices: 22.6 us -> 13.5 us
  waiting for transfers between devices: 23.1 us -> 31.8 us
  local copies, waits for them, and re-layouts: 5.36 us -> 7.02 us
  between operations: 10.4 us -> 9.65 us
    ppermute x19 -> x12, starting transfers between devices: 22.6 us -> 13.5 us  [swap(): return lax.ppermute(value, axis, [(i, i ^ bit) for i in range(size)])]
    ppermute x19 -> x12, waiting for transfers between devices: 23.1 us -> 31.8 us  [swap(): return lax.ppermute(value, axis, [(i, i ^ bit) for i in range(size)])]
    another operation x0 -> x1, other arithmetic: none -> 1.87 us  [per_device(): downs = jnp.stack([query_down, value_down], axis=1)]
    convert_element_type x1, other arithmetic: 1.14 us -> 0.1 us  [per_device(): query_base[0][:, None, :]]
    unnamed x15 -> x12, local copies, waits for them, and re-layouts: 0.98 us -> 1.93 us
    select_n x4 -> x2, other arithmetic: 2.95 us -> 2.13 us  [select_members(): slots.append(jnp.where(m // row_span == row, near, received[s]))]
    concatenate x0 -> x1, local copies, waits for them, and re-layouts: none -> 0.76 us  [per_device(): ups = jnp.concatenate([query_up, value_raise_factor], axis=2)]
    select_n x3 -> x2, other arithmetic: 2.11 us -> 2.12 us  [pick(): return jnp.where(index // local_count == core, mine, theirs)]
  transfers between devices with their start and end apart: 19 -> 12, of which waited for: 6 -> 6; matrix products, arithmetic and copies ran while one was open for 22% -> 23% of each run, Pallas kernels for 0% -> 0%
where the time goes in v2:
time: 74.6 us; the launch traced here: 74 us
  waiting for transfers between devices  31.8 us (43%)
  starting transfers between devices  13.5 us (18%)
  between operations  9.65 us (13%)
  other arithmetic  9.64 us (13%)
  local copies, waits for them, and re-layouts  7.02 us (9%)
  matrix products  2.51 us (3%)
    ppermute x12, waiting for transfers between devices, swap(): return lax.ppermute(value, axis, [(i, i ^ bit) for i in range(size)])  31.8 us
    ppermute x12, starting transfers between devices, swap(): return lax.ppermute(value, axis, [(i, i ^ bit) for i in range(size)])  13.5 us
    select_n x2, other arithmetic, select_members(): slots.append(jnp.where(m // row_span == row, near, received[s]))  2.13 us
    select_n x2, other arithmetic, pick(): return jnp.where(index // local_count == core, mine, theirs)  2.12 us
    unnamed x12, local copies, waits for them, and re-layouts  1.93 us
    another operation x1, other arithmetic, per_device(): downs = jnp.stack([query_down, value_down], axis=1)  1.87 us
  transfers between devices with their start and end apart: 12, of which 6 were waited for; matrix products, arithmetic and copies ran while one was open for 23% of the time, Pallas kernels for 0%

profile of v2, /device:TPU:0, one launch (start us, length us, event | category | flops | bytes accessed | tf_op | source)
XLA Modules:
  0.0 74.0 jit_solution(10953236327487736922)
XLA Ops:
  0.0 3.0 %collective-permute-start.2 = (s32[1,2]{1,0:T(1,128)}, s32[1,2]{1,0:T(1,128)S(1)}, u32[]{:S(2)}, u32[]{:S(2)}) collective-permute-start(s32[1,2]{1,0:T(1,128)} %param.18), channel_id=1, source_target_pairs={{0,8},{4,12},{8,0},{12,4},{1,9},{5,13},{9,1},{13,5},{2,10},{6,14},... | collective-permute-start | bytes 32 | tf_op jit(solution)/shard_map/ppermute | solution.py:22
  3.0 0.9 %copy.18 = bf16[1,128,256]{1,2,0:T(8,128)(2,1)S(1)} copy(bf16[1,128,256]{2,1,0:T(8,128)(2,1)} %param.12) | data formatting | bytes 131072 | tf_op args[2]
  4.0 1.6 %collective-permute-start = (bf16[128,256]{0,1:T(8,128)(2,1)S(1)}, bf16[128,256]{0,1:T(8,128)(2,1)}, u32[]{:S(2)}, u32[]{:S(2)}) collective-permute-start(bf16[128,256]{0,1:T(8,128)(2,1)S(1)} %bitcast.94), channel_id=1, source_target_pairs={{0,16},{16,0},{1,17},{17,1},{2,18},{18,2},{3,19},{19,3},{4,20},{20... | collective-permute-start | bytes 196616 | tf_op jit(solution)/shard_map/ppermute | solution.py:22
  5.5 1.0 %constant_dynamic-update-slice_fusion.1 = bf16[2,32,2304]{2,1,0:T(8,128)(2,1)S(1)} fusion(bf16[2,32,2048]{2,1,0:T(8,128)(2,1)} %param.15), kind=kLoop, calls=%fused_computation.76 | loop fusion | bytes 524288
  6.5 0.8 %constant_dynamic-update-slice_fusion = bf16[2,32,2304]{2,1,0:T(8,128)(2,1)S(1)} fusion(bf16[2,32,2304]{2,1,0:T(8,128)(2,1)S(1)} %constant_dynamic-update-slice_fusion.1, bf16[2,32,256]{2,1,0:T(8,128)(2,1)} %param.17), kind=kLoop, calls=%fused_computation.75 | loop fusion | bytes 65536 | tf_op jit(solution)/shard_map/concatenate | solution.py:101
  7.2 0.0 collective-permute-start.1
  7.2 1.9 %pad_maximum_fusion = bf16[2,2,32,2048]{3,2,1,0:T(8,128)(2,1)} fusion(bf16[2,1,32,2048]{3,2,1,0:T(8,128)(2,1)} %bitcast.87, bf16[2,1,32,2048]{3,2,1,0:T(8,128)(2,1)} %bitcast.84), kind=kLoop, calls=%fused_computation.28 | loop fusion | flops 262144 | bytes 1048576 | tf_op jit(solution)/shard_map/stack | solution.py:100
  9.1 0.5 collective-permute-start.5
  9.6 1.3 %fusion.40 = (s32[1,1]{1,0:T(1,128)}, s32[1,1]{1,0:T(1,128)}) fusion(s32[1,2]{1,0:T(1,128)} %param.18), kind=kLoop, calls=%fused_computation.81 | loop fusion | bytes 16 | tf_op jit(solution)/shard_map/slice | solution.py:77
  16.8 0.9 %bitcast_convert_fusion.1 = f32[128,256]{1,0:T(8,128)S(1)} fusion(bf16[1,128,256]{2,1,0:T(8,128)(2,1)} %param.13), kind=kLoop, calls=%fused_computation.67 | loop fusion | flops 32768 | bytes 196608 | tf_op jit(solution)/shard_map/convert_element_type | solution.py:160
  17.6 0.8 %copy.23 = f32[128,256]{0,1:T(8,128)} copy(f32[128,256]{1,0:T(8,128)S(1)} %bitcast_convert_fusion.1) | data formatting | bytes 262144 | tf_op jit(solution)/shard_map/convert_element_type | solution.py:160
  18.4 0.1 bitcast_convert_fusion
  18.5 0.3 copy.19
  18.8 0.1 fusion.32
  18.9 0.0 collective-permute-done.2
  18.9 0.6 fusion.41
  23.2 0.0 collective-permute-done
  23.2 0.9 %broadcast_select_fusion.3 = (bf16[128,256]{0,1:T(8,128)(2,1)S(1)}, bf16[128,256]{0,1:T(8,128)(2,1)S(1)}) fusion(bf16[128,256]{0,1:T(8,128)(2,1)} %collective-permute-done, pred[]{:T(512)S(6)} %eq.54, bf16[1,128,256]{1,2,0:T(8,128)(2,1)S(1)} %copy.18), kind=kLoop, calls=%fused_computation.69 | loop fusion | flops 65536 | bytes 262145 | tf_op jit(solution)/shard_map/jit(_where)/select_n | solution.py:31
  24.0 0.0 collective-permute-done.5
  24.1 1.1 %fusion.26 = (bf16[1,2,32,2048]{3,2,1,0:T(8,128)(2,1)S(1)}, bf16[1,2,32,2048]{3,2,1,0:T(8,128)(2,1)S(1)}) fusion(s32[]{:T(128)S(6)} %select_n.266, bf16[2,1,32,2048]{3,2,1,0:T(8,128)(2,1)S(1)} %bitcast.85, bf16[2,1,32,2048]{3,2,1,0:T(8,128)(2,1)S(1)} %bitcast.88, bf16[2,2,32,2048]{3,2,1,0:T(8,128)(2,1)} %collective-permute-done.5, pred[]{:T(512)S(6)} %eq.57, ...), kind=kLoop, calls=%fused_computation.45 | loop fusion | flops 524288 | bytes 1572874 | tf_op jit(solution)/shard_map/jit(_where)/select_n | solution.py:66
  25.2 0.1 pad_maximum_fusion.2
  25.2 0.6 collective-permute-start.6
  25.8 0.0 collective-permute-done.1
  25.8 1.0 %dynamic-slice_select_fusion.1 = (bf16[1,32,2304]{2,1,0:T(8,128)(2,1)S(1)}, bf16[1,32,2304]{2,1,0:T(8,128)(2,1)S(1)}) fusion(bf16[2,32,2304]{2,1,0:T(8,128)(2,1)} %collective-permute-done.1, s32[]{:T(128)S(6)} %select_n.266, bf16[2,32,2304]{2,1,0:T(8,128)(2,1)S(1)} %constant_dynamic-update-slice_fusion, pred[]{:T(512)S(6)} %eq.57, s32[]{:T(128)S(6)} %select_n.272, ...), kind=kLoop, calls=%fused_computation.55 | loop fusion | flops 147456 | bytes 884746 | tf_op jit(solution)/shard_map/jit(_where)/select_n | solution.py:66
  26.9 1.6 %collective-permute-start.3 = (bf16[2,32,2304]{2,1,0:T(8,128)(2,1)S(1)}, bf16[2,32,2304]{2,1,0:T(8,128)(2,1)S(1)}, u32[]{:S(2)}, u32[]{:S(2)}) collective-permute-start(bf16[2,32,2304]{2,1,0:T(8,128)(2,1)S(1)} %pad_maximum_fusion.4), channel_id=1, source_target_pairs={{0,8},{4,12},{8,0},{12,4},{1,9},{5,13},{9,1},{13,5},{2,10},{6,14},... | collective-permute-start | bytes 884744 | tf_op jit(solution)/shard_map/ppermute | solution.py:22
  28.4 11.6 %collective-permute-done.6 = bf16[2,2,32,2048]{3,2,1,0:T(8,128)(2,1)S(1)} collective-permute-done((bf16[2,2,32,2048]{3,2,1,0:T(8,128)(2,1)S(1)}, bf16[2,2,32,2048]{3,2,1,0:T(8,128)(2,1)S(1)}, u32[]{:S(2)}, u32[]{:S(2)}) %collective-permute-start.6) | collective-permute-done | bytes 524320 | tf_op jit(solution)/shard_map/ppermute | solution.py:22
  40.1 1.1 %fusion.24 = (bf16[1,2,32,2048]{3,2,1,0:T(8,128)(2,1)S(1)}, bf16[1,2,32,2048]{3,2,1,0:T(8,128)(2,1)S(1)}) fusion(s32[]{:T(128)S(6)} %select_n.260, bf16[2,1,32,2048]{3,2,1,0:T(8,128)(2,1)S(1)} %bitcast.86, bf16[2,1,32,2048]{3,2,1,0:T(8,128)(2,1)S(1)} %bitcast.89, bf16[2,2,32,2048]{3,2,1,0:T(8,128)(2,1)S(1)} %collective-permute-done.6, ...), kind=kLoop, calls=%fused_computation.43 | loop fusion | flops 786432 | bytes 2097164 | tf_op jit(solution)/shard_map/jit(_where)/select_n | solution.py:79
  41.2 0.1 pad_maximum_fusion.3
  41.2 0.6 collective-permute-start.7
  41.8 3.6 %collective-permute-done.3 = bf16[2,32,2304]{2,1,0:T(8,128)(2,1)S(1)} collective-permute-done((bf16[2,32,2304]{2,1,0:T(8,128)(2,1)S(1)}, bf16[2,32,2304]{2,1,0:T(8,128)(2,1)S(1)}, u32[]{:S(2)}, u32[]{:S(2)}) %collective-permute-start.3) | collective-permute-done | bytes 294944 | tf_op jit(solution)/shard_map/ppermute | solution.py:22
  45.4 1.0 %slice_select_fusion.1 = (bf16[1,32,2304]{2,1,0:T(8,128)(2,1)S(1)}, bf16[1,32,2304]{2,1,0:T(8,128)(2,1)S(1)}) fusion(bf16[2,32,2304]{2,1,0:T(8,128)(2,1)S(1)} %collective-permute-done.3, bf16[2,32,2304]{2,1,0:T(8,128)(2,1)} %collective-permute-done.1, s32[]{:T(128)S(6)} %select_n.260, bf16[2,32,2304]{2,1,0:T(8,128)(2,1)S(1)} %constant_dynamic-update-slice_fusion, ...), kind=kLoop, calls=%fused_computation.53 | loop fusion | flops 294912 | bytes 1179660 | tf_op jit(solution)/shard_map/jit(_where)/select_n | solution.py:79
  46.5 0.6 collective-permute-start.4
  47.1 9.0 %collective-permute-done.7 = bf16[2,2,32,2048]{3,2,1,0:T(8,128)(2,1)S(1)} collective-permute-done((bf16[2,2,32,2048]{3,2,1,0:T(8,128)(2,1)S(1)}, bf16[2,2,32,2048]{3,2,1,0:T(8,128)(2,1)S(1)}, u32[]{:S(2)}, u32[]{:S(2)}) %collective-permute-start.7) | collective-permute-done | bytes 524320 | tf_op jit(solution)/shard_map/ppermute | solution.py:22
  56.1 0.4 convolution_bitcast_fusion.2
  56.6 3.7 %collective-permute-start.10 = (f32[128,2,2,64]{0,3,1,2:T(8,128)S(1)}, f32[128,2,2,64]{0,3,1,2:T(8,128)S(1)}, u32[]{:S(2)}, u32[]{:S(2)}) collective-permute-start(f32[128,2,2,64]{0,3,1,2:T(8,128)S(1)} %convolution_bitcast_fusion.2), channel_id=1, source_target_pairs={{0,3},{1,2},{2,1},{3,0},{4,7},{5,6},{6,5},{7,4},{8,11},{9,10},{10,... | collective-permute-start | bytes 393224 | tf_op jit(solution)/shard_map/ppermute | solution.py:22
  60.2 0.0 collective-permute-start.9
  60.2 0.8 %collective-permute-start.8 = (f32[128,2,2,64]{0,3,1,2:T(8,128)S(1)}, f32[128,2,2,64]{0,3,1,2:T(8,128)S(1)}, u32[]{:S(2)}, u32[]{:S(2)}) collective-permute-start(f32[128,2,2,64]{0,3,1,2:T(8,128)S(1)} %convolution_bitcast_fusion.2), channel_id=1, source_target_pairs={{0,1},{1,0},{2,3},{3,2},{4,5},{5,4},{6,7},{7,6},{8,9},{9,8},{10,11... | collective-permute-start | bytes 393224 | tf_op jit(solution)/shard_map/ppermute | solution.py:22
  61.0 0.0 collective-permute-done.4
  61.1 2.4 %collective-permute-done.10 = f32[128,2,2,64]{0,3,1,2:T(8,128)S(1)} collective-permute-done((f32[128,2,2,64]{0,3,1,2:T(8,128)S(1)}, f32[128,2,2,64]{0,3,1,2:T(8,128)S(1)}, u32[]{:S(2)}, u32[]{:S(2)}) %collective-permute-start.10) | collective-permute-done | bytes 131104 | tf_op jit(solution)/shard_map/ppermute | solution.py:22
  63.5 3.3 %collective-permute-done.9 = f32[128,2,2,64]{0,3,1,2:T(8,128)S(1)} collective-permute-done((f32[128,2,2,64]{0,3,1,2:T(8,128)S(1)}, f32[128,2,2,64]{0,3,1,2:T(8,128)S(1)}, u32[]{:S(2)}, u32[]{:S(2)}) %collective-permute-start.9) | collective-permute-done | bytes 131104 | tf_op jit(solution)/shard_map/ppermute | solution.py:22
  66.9 0.2 fusion.12
  67.1 0.6 collective-permute-start.11
  67.7 0.5 fusion.4
  68.2 0.8 %fusion = (f32[2,2,8,128]{3,2,0,1:T(8,128)S(1)}, f32[2,256,128,2,8]{2,1,4,3,0:T(8,128)S(1)}) fusion(pred[128,256]{0,1:T(8,128)(4,1)S(1)} %fusion.32, bf16[256,2,128,1,1]{0,2,4,3,1:T(8,128)(2,1)S(1)} %bitcast.92, bf16[128,2,2,8,128]{0,4,3,2,1:T(8,128)(2,1)S(1)} %bitcast.83), kind=kOutput, calls=%fused_computation.2 | convolution fusion | flops 271577088 | bytes 5423104 | tf_op jit(solution)/shard_map/while/body/eval_jaxpr/rsgjd,kgd->sgjrk/dot_general | solution.py:131
  69.1 1.3 %fusion.1 = (f32[2,2,8,128]{3,2,0,1:T(8,128)S(1)}, bf16[2,2,8,128,256]{3,4,2,0,1:T(8,128)(2,1)S(1)}) fusion(f32[2,256,128,2,8]{2,1,4,3,0:T(8,128)S(1)} %get-tuple-element.56, f32[2,2,8,128]{3,2,0,1:T(8,128)S(1)} %get-tuple-element.50, pred[128,256]{0,1:T(8,128)(4,1)S(1)} %fusion.32), kind=kLoop, calls=%fused_computation.3 | loop fusion | flops 6287360 | bytes 6356992 | tf_op jit(solution)/shard_map/while/body/eval_jaxpr/reduce_sum | solution.py:144
  70.4 1.8 %collective-permute-done.11 = bf16[128,512]{0,1:T(8,128)(2,1)S(1)} collective-permute-done((bf16[128,512]{0,1:T(8,128)(2,1)S(1)}, bf16[128,512]{0,1:T(8,128)(2,1)S(1)}, u32[]{:S(2)}, u32[]{:S(2)}) %collective-permute-start.11) | collective-permute-done | bytes 131104 | tf_op jit(solution)/shard_map/ppermute | solution.py:22
  72.2 0.5 fusion.6
  72.7 1.3 %copy.26 = bf16[2,1,128,2048]{3,2,1,0:T(8,128)(2,1)} copy(bf16[2,1,128,2048]{2,3,0,1:T(8,128)(2,1)S(1)} %bitcast.90) | data formatting | bytes 2097152 | tf_op jit(solution)/shard_map/convert_element_type | solution.py:180
  (22 shorter events, 0.3 us)
Async XLA Ops:
  0.0 56.1 %copy-start = (bf16[1,128,2048]{2,1,0:T(8,128)(2,1)S(1)}, bf16[1,128,2048]{2,1,0:T(8,128)(2,1)}, u32[]{:S(2)}) copy-start(bf16[1,128,2048]{2,1,0:T(8,128)(2,1)} %param.10) | copy-start | bytes 1572868
  0.0 18.4 %copy-start.3 = (bf16[1,128,2048]{2,1,0:T(8,128)(2,1)S(1)}, bf16[1,128,2048]{2,1,0:T(8,128)(2,1)}, u32[]{:S(2)}) copy-start(bf16[1,128,2048]{2,1,0:T(8,128)(2,1)} %param.11) | copy-start | bytes 1572868
  0.0 18.9 %collective-permute-start.2 = (s32[1,2]{1,0:T(1,128)}, s32[1,2]{1,0:T(1,128)S(1)}, u32[]{:S(2)}, u32[]{:S(2)}) collective-permute-start(s32[1,2]{1,0:T(1,128)} %param.18), channel_id=1, source_target_pairs={{0,8},{4,12},{8,0},{12,4},{1,9},{5,13},{9,1},{13,5},{2,10},{6,14},... | collective-permute-start | bytes 32 | tf_op jit(solution)/shard_map/ppermute | solution.py:22
  4.0 19.2 %collective-permute-start = (bf16[128,256]{0,1:T(8,128)(2,1)S(1)}, bf16[128,256]{0,1:T(8,128)(2,1)}, u32[]{:S(2)}, u32[]{:S(2)}) collective-permute-start(bf16[128,256]{0,1:T(8,128)(2,1)S(1)} %bitcast.94), channel_id=1, source_target_pairs={{0,16},{16,0},{1,17},{17,1},{2,18},{18,2},{3,19},{19,3},{4,20},{20... | collective-permute-start | bytes 196616 | tf_op jit(solution)/shard_map/ppermute | solution.py:22
  7.2 18.5 %collective-permute-start.1 = (bf16[2,32,2304]{2,1,0:T(8,128)(2,1)S(1)}, bf16[2,32,2304]{2,1,0:T(8,128)(2,1)}, u32[]{:S(2)}, u32[]{:S(2)}) collective-permute-start(bf16[2,32,2304]{2,1,0:T(8,128)(2,1)S(1)} %constant_dynamic-update-slice_fusion), channel_id=1, source_target_pairs={{0,4},{4,0},{8,12},{12,8},{1,5},{5,1},{9,13},{13,9},{2,6},{6,2},{1... | collective-permute-start | bytes 884744 | tf_op jit(solution)/shard_map/ppermute | solution.py:22
  9.1 14.9 %collective-permute-start.5 = (bf16[2,2,32,2048]{3,2,1,0:T(8,128)(2,1)}, bf16[2,2,32,2048]{3,2,1,0:T(8,128)(2,1)}, u32[]{:S(2)}, u32[]{:S(2)}) collective-permute-start(bf16[2,2,32,2048]{3,2,1,0:T(8,128)(2,1)} %pad_maximum_fusion), channel_id=1, source_target_pairs={{0,4},{4,0},{8,12},{12,8},{1,5},{5,1},{9,13},{13,9},{2,6},{6,2},{1... | collective-permute-start | bytes 1572872 | tf_op jit(solution)/shard_map/ppermute | solution.py:22
  18.4 5.7 %copy-start.1 = (bf16[2,32,2048]{2,1,0:T(8,128)(2,1)S(1)}, bf16[2,32,2048]{2,1,0:T(8,128)(2,1)}, u32[]{:S(2)}) copy-start(bf16[2,32,2048]{2,1,0:T(8,128)(2,1)} %param.14) | copy-start | bytes 786436
  18.4 5.7 %copy-start.2 = (bf16[2,32,2048]{2,1,0:T(8,128)(2,1)S(1)}, bf16[2,32,2048]{2,1,0:T(8,128)(2,1)}, u32[]{:S(2)}) copy-start(bf16[2,32,2048]{2,1,0:T(8,128)(2,1)} %param.16) | copy-start | bytes 786436
  25.2 14.9 %collective-permute-start.6 = (bf16[2,2,32,2048]{3,2,1,0:T(8,128)(2,1)S(1)}, bf16[2,2,32,2048]{3,2,1,0:T(8,128)(2,1)S(1)}, u32[]{:S(2)}, u32[]{:S(2)}) collective-permute-start(bf16[2,2,32,2048]{3,2,1,0:T(8,128)(2,1)S(1)} %pad_maximum_fusion.2), channel_id=1, source_target_pairs={{0,8},{4,12},{8,0},{12,4},{1,9},{5,13},{9,1},{13,5},{2,10},{6,14},... | collective-permute-start | bytes 1572872 | tf_op jit(solution)/shard_map/ppermute | solution.py:22
  26.9 18.6 %collective-permute-start.3 = (bf16[2,32,2304]{2,1,0:T(8,128)(2,1)S(1)}, bf16[2,32,2304]{2,1,0:T(8,128)(2,1)S(1)}, u32[]{:S(2)}, u32[]{:S(2)}) collective-permute-start(bf16[2,32,2304]{2,1,0:T(8,128)(2,1)S(1)} %pad_maximum_fusion.4), channel_id=1, source_target_pairs={{0,8},{4,12},{8,0},{12,4},{1,9},{5,13},{9,1},{13,5},{2,10},{6,14},... | collective-permute-start | bytes 884744 | tf_op jit(solution)/shard_map/ppermute | solution.py:22
  41.2 14.9 %collective-permute-start.7 = (bf16[2,2,32,2048]{3,2,1,0:T(8,128)(2,1)S(1)}, bf16[2,2,32,2048]{3,2,1,0:T(8,128)(2,1)S(1)}, u32[]{:S(2)}, u32[]{:S(2)}) collective-permute-start(bf16[2,2,32,2048]{3,2,1,0:T(8,128)(2,1)S(1)} %pad_maximum_fusion.3), channel_id=1, source_target_pairs={{0,16},{16,0},{1,17},{17,1},{2,18},{18,2},{3,19},{19,3},{4,20},{20... | collective-permute-start | bytes 1572872 | tf_op jit(solution)/shard_map/ppermute | solution.py:22
  46.5 14.5 %collective-permute-start.4 = (bf16[2,32,2304]{2,1,0:T(8,128)(2,1)S(1)}, bf16[2,32,2304]{2,1,0:T(8,128)(2,1)S(1)}, u32[]{:S(2)}, u32[]{:S(2)}) collective-permute-start(bf16[2,32,2304]{2,1,0:T(8,128)(2,1)S(1)} %pad_maximum_fusion.5), channel_id=1, source_target_pairs={{0,16},{16,0},{1,17},{17,1},{2,18},{18,2},{3,19},{19,3},{4,20},{20... | collective-permute-start | bytes 884744 | tf_op jit(solution)/shard_map/ppermute | solution.py:22
  47.1 19.7 %copy-start.4 = (f32[128,256]{0,1:T(8,128)S(1)}, f32[128,256]{0,1:T(8,128)}, u32[]{:S(2)}) copy-start(f32[128,256]{0,1:T(8,128)} %copy.23) | copy-start | bytes 393220
  56.6 6.9 %collective-permute-start.10 = (f32[128,2,2,64]{0,3,1,2:T(8,128)S(1)}, f32[128,2,2,64]{0,3,1,2:T(8,128)S(1)}, u32[]{:S(2)}, u32[]{:S(2)}) collective-permute-start(f32[128,2,2,64]{0,3,1,2:T(8,128)S(1)} %convolution_bitcast_fusion.2), channel_id=1, source_target_pairs={{0,3},{1,2},{2,1},{3,0},{4,7},{5,6},{6,5},{7,4},{8,11},{9,10},{10,... | collective-permute-start | bytes 393224 | tf_op jit(solution)/shard_map/ppermute | solution.py:22
  60.2 6.6 %collective-permute-start.9 = (f32[128,2,2,64]{0,3,1,2:T(8,128)S(1)}, f32[128,2,2,64]{0,3,1,2:T(8,128)S(1)}, u32[]{:S(2)}, u32[]{:S(2)}) collective-permute-start(f32[128,2,2,64]{0,3,1,2:T(8,128)S(1)} %convolution_bitcast_fusion.2), channel_id=1, source_target_pairs={{0,2},{1,3},{2,0},{3,1},{4,6},{5,7},{6,4},{7,5},{8,10},{9,11},{10,... | collective-permute-start | bytes 393224 | tf_op jit(solution)/shard_map/ppermute | solution.py:22
  60.2 6.6 %collective-permute-start.8 = (f32[128,2,2,64]{0,3,1,2:T(8,128)S(1)}, f32[128,2,2,64]{0,3,1,2:T(8,128)S(1)}, u32[]{:S(2)}, u32[]{:S(2)}) collective-permute-start(f32[128,2,2,64]{0,3,1,2:T(8,128)S(1)} %convolution_bitcast_fusion.2), channel_id=1, source_target_pairs={{0,1},{1,0},{2,3},{3,2},{4,5},{5,4},{6,7},{7,6},{8,9},{9,8},{10,11... | collective-permute-start | bytes 393224 | tf_op jit(solution)/shard_map/ppermute | solution.py:22
  67.1 5.0 %collective-permute-start.11 = (bf16[128,512]{0,1:T(8,128)(2,1)S(1)}, bf16[128,512]{0,1:T(8,128)(2,1)S(1)}, u32[]{:S(2)}, u32[]{:S(2)}) collective-permute-start(bf16[128,512]{0,1:T(8,128)(2,1)S(1)} %bitcast.91), channel_id=1, source_target_pairs={{0,16},{16,0},{1,17},{17,1},{2,18},{18,2},{3,19},{19,3},{4,20},{20... | collective-permute-start | bytes 393224 | tf_op jit(solution)/shard_map/ppermute | solution.py:22

commit v3 on v2

v3 whole, which is shorter than its diff:
```python
import math

import jax
import jax.numpy as jnp
from jax import lax
from jax.sharding import PartitionSpec as P

HEAD_SIZE = 128


def block_rows(total_rows):
    if total_rows <= 512:
        return total_rows
    for candidate in range(512, 0, -1):
        if total_rows % candidate == 0:
            return candidate
    return total_rows


def swap(value, axis, bit):
    size = lax.axis_size(axis)
    return lax.ppermute(value, axis, [(i, i ^ bit) for i in range(size)])


def ctx_gather(mine, dim, ordered):
    if lax.axis_size("ctx") == 2:
        other = swap(mine, "ctx", 1)
        if not ordered:
            return jnp.concatenate([mine, other], axis=dim)
        first = lax.axis_index("ctx") == 0
        low = jnp.where(first, mine, other)
        high = jnp.where(first, other, mine)
        return jnp.concatenate([low, high], axis=dim)
    return lax.all_gather(mine, "ctx", axis=dim, tiled=True)


def mp_sum(value):
    size = lax.axis_size("mp")
    if size & (size - 1):
        return lax.psum(value, "mp")
    total = value
    for bit in range(1, size):
        total = total + swap(value, "mp", bit)
    return total


def select_members(factor_set, member_ids, member_lists):
    local_count = factor_set[0].shape[0]
    req_size = lax.axis_size("req")
    if req_size != 4:
        everything = [lax.all_gather(f, "req", axis=0, tiled=True) for f in factor_set]
        return [
            jnp.stack([lax.dynamic_index_in_dim(f, m, 0, keepdims=False) for m in member_ids])
            for f in everything
        ]
    req = lax.axis_index("req")
    core = req % 2
    row = req // 2
    row_span = 2 * local_count
    partners = swap(tuple(factor_set), "req", 1)
    far_ids = swap(member_lists, "req", 2)[0]

    def pick(own, partner, index):
        mine = lax.dynamic_index_in_dim(own, index % local_count, 0, keepdims=False)
        theirs = lax.dynamic_index_in_dim(partner, index % local_count, 0, keepdims=False)
        return jnp.where(index // local_count == core, mine, theirs)

    outgoing = tuple(
        jnp.stack([pick(own, partner, far_ids[s] % row_span) for s in range(far_ids.shape[0])])
        for own, partner in zip(factor_set, partners)
    )
    incoming = swap(outgoing, "req", 2)
    chosen = []
    for own, partner, received in zip(factor_set, partners, incoming):
        slots = []
        for s in range(member_ids.shape[0]):
            m = member_ids[s]
            near = pick(own, partner, m % row_span)
            slots.append(jnp.where(m // row_span == row, near, received[s]))
        chosen.append(jnp.stack(slots))
    return chosen


def attend(grouped, keys, values, key_positions, positions, live_length, slot_count):
    row_count, _, group_count, group_portion, _ = grouped.shape
    inverse = 1.0 / math.sqrt(HEAD_SIZE)

    def update(running, key_block, value_block, block_positions):
        run_max, run_total, accumulated = running
        block_length = key_block.shape[0]
        heads_of_keys = key_block.reshape(block_length, group_count, HEAD_SIZE)
        heads_of_values = value_block.reshape(block_length, slot_count, group_count, HEAD_SIZE)
        scores = (
            jnp.einsum(
                "rsgjd,kgd->sgjrk", grouped, heads_of_keys, preferred_element_type=jnp.float32
            )
            * inverse
        )
        visible = (block_positions[None, :] <= positions[:, None]) & (
            block_positions[None, :] < live_length
        )
        masked = jnp.where(visible, scores, -1e30)
        new_max = jnp.maximum(run_max, jnp.max(masked, axis=-1))
        weights = jnp.where(visible, jnp.exp(masked - new_max[..., None]), 0.0)
        factor = jnp.exp(run_max - new_max)
        new_total = run_total * factor + jnp.sum(weights, axis=-1)
        new_accumulated = accumulated * factor[..., None] + jnp.einsum(
            "sgjrk,ksgd->sgjrd",
            weights.astype(jnp.bfloat16),
            heads_of_values,
            preferred_element_type=jnp.float32,
        )
        return (new_max, new_total, new_accumulated)

    initial = (
        jnp.full((slot_count, group_count, group_portion, row_count), -1e30, jnp.float32),
        jnp.zeros((slot_count, group_count, group_portion, row_count), jnp.float32),
        jnp.zeros((slot_count, group_count, group_portion, row_count, HEAD_SIZE), jnp.float32),
    )
    piece_rows = keys.shape[0]
    step_rows = block_rows(piece_rows)

    def advance(block_index, current):
        offset = block_index * step_rows
        key_block = lax.dynamic_slice_in_dim(keys, offset, step_rows, 0)
        value_block = lax.dynamic_slice_in_dim(values, offset, step_rows, 0)
        block_positions = lax.dynamic_slice_in_dim(key_positions, offset, step_rows, 0)
        return update(current, key_block, value_block, block_positions)

    run_max, run_total, accumulated = lax.fori_loop(0, piece_rows // step_rows, advance, initial)
    result = accumulated / run_total[..., None]
    return (
        jnp.transpose(result, (0, 3, 1, 2, 4))
        .reshape(slot_count, row_count, group_count * group_portion * HEAD_SIZE)
        .astype(jnp.bfloat16)
    )


def per_device(
    activations,
    query_base,
    key_base,
    plain_value_rows,
    query_down,
    query_up,
    value_down,
    value_raise_factor,
    member_lists,
    prompt_lengths,
):
    row_count = activations.shape[1]
    member_ids = member_lists[0]
    slot_count = member_ids.shape[0]
    up_width = query_up.shape[2]
    group_count = key_base.shape[2] // HEAD_SIZE
    ctx = lax.axis_index("ctx")
    positions = ctx * row_count + jnp.arange(row_count, dtype=jnp.int32)
    downs = jnp.stack([query_down, value_down], axis=1)
    ups = jnp.concatenate([query_up, value_raise_factor], axis=2)
    down_half, up_half = select_members((downs, ups), member_ids, member_lists)
    ups = ctx_gather(up_half, 1, False)
    up_query = ups[..., :up_width]
    up_value = ups[..., up_width:]
    if lax.axis_size("ctx") == 2:
        tokens = ctx_gather(activations[0], 0, False)
        partial = jnp.einsum("rd,sfkd->rfsk", tokens, down_half, preferred_element_type=jnp.float32)
        mine = mp_sum(partial).astype(jnp.bfloat16)
        theirs = swap(mine, "ctx", 1)
        theirs = jnp.concatenate([theirs[row_count:], theirs[:row_count]], axis=0)
        ranks = jnp.concatenate([mine, theirs], axis=3)
        value_rows = ctx_gather(plain_value_rows[0], 0, False)
        keys = ctx_gather(key_base[0], 0, False)
        own_keys = jnp.arange(row_count, dtype=jnp.int32)
        key_positions = jnp.concatenate(
            [ctx * row_count + own_keys, (1 - ctx) * row_count + own_keys]
        )
        rank_query = ranks[:row_count, 0]
        rank_value = ranks[:, 1]
    else:
        downs = ctx_gather(down_half, 2, False)
        partial = jnp.einsum(
            "rd,sfkd->rfsk", activations[0], downs, preferred_element_type=jnp.float32
        )
        ranks = mp_sum(partial).astype(jnp.bfloat16)
        rank_query = ranks[:, 0]
        rank_value = ranks[:, 1]
        value_rows = plain_value_rows[0]
        keys = ctx_gather(key_base[0], 0, True)
        key_positions = jnp.arange(keys.shape[0], dtype=jnp.int32)
    query_matrix = (
        query_base[0][:, None, :]
        + jnp.einsum("rsk,skc->rsc", rank_query, up_query, preferred_element_type=jnp.float32)
    ).astype(jnp.bfloat16)
    group_portion = query_matrix.shape[2] // (group_count * HEAD_SIZE)
    grouped = query_matrix.reshape(row_count, slot_count, group_count, group_portion, HEAD_SIZE)
    built = (
        value_rows[:, None, :]
        + jnp.einsum("rsk,skc->rsc", rank_value, up_value, preferred_element_type=jnp.float32)
    ).astype(jnp.bfloat16)
    values = built.reshape(built.shape[0], slot_count * group_count * HEAD_SIZE)
    if lax.axis_size("ctx") != 2:
        values = ctx_gather(values, 0, True)
    result = attend(
        grouped, keys, values, key_positions, positions, prompt_lengths[0], slot_count
    )
    return result[:, None]


def solution(mesh):
    in_specs = (
        P("req", "ctx", "mp"),
        P("req", "ctx", "mp"),
        P("req", "ctx", "mp"),
        P("req", "ctx", "mp"),
        P("req", "ctx", "mp"),
        P("req", "ctx", "mp"),
        P("req", "ctx", "mp"),
        P("req", "ctx", "mp"),
        P("req", None),
        P("req"),
    )
    out_specs = P(None, "req", "ctx", "mp")
    return jax.shard_map(
        per_device, mesh=mesh, in_specs=in_specs, out_specs=out_specs, check_vma=False
    )
```

time: 74.6 us -> 71.5 us (0.958)
  waiting for transfers between devices: 31.8 us -> 27 us
  other arithmetic: 9.64 us -> 6.67 us
  local copies, waits for them, and re-layouts: 7.02 us -> 8.96 us
  starting transfers between devices: 13.5 us -> 14.9 us
  matrix products: 2.51 us -> 3.58 us
    ppermute x12 -> x13, waiting for transfers between devices: 31.8 us -> 27 us  [swap(): return lax.ppermute(value, axis, [(i, i ^ bit) for i in range(size)])]
    concatenate x0 -> x2, local copies, waits for them, and re-layouts: none -> 1.9 us  [ctx_gather(): return jnp.concatenate([mine, other], axis=dim)]
    ppermute x12 -> x13, starting transfers between devices: 13.5 us -> 14.9 us  [swap(): return lax.ppermute(value, axis, [(i, i ^ bit) for i in range(size)])]
    dot_general x1, matrix products: 0.43 us -> 1.53 us  [per_device(): jnp.einsum('rd,sfkd->rfsk', tokens, down_half, preferred_element_type=jnp...]
    select_n x2, other arithmetic: 2.13 us -> 1.1 us  [select_members(): slots.append(jnp.where(m // row_span == row, near, received[s]))]
    select_n x2, other arithmetic: 2.12 us -> 1.09 us  [pick(): return jnp.where(index // local_count == core, mine, theirs)]
    select_n x2 -> x0, other arithmetic: 0.88 us -> none  [ctx_gather(): low = jnp.where(first, mine, other)]
  transfers between devices with their start and end apart: 12 -> 13, of which waited for: 6 -> 5; matrix products, arithmetic and copies ran while one was open for 23% -> 20% of each run, Pallas kernels for 0% -> 0%
where the time goes in v3:
time: 71.5 us; the launch traced here: 70.9 us
  waiting for transfers between devices  27 us (38%)
  starting transfers between devices  14.9 us (21%)
  between operations  9.8 us (14%)
  local copies, waits for them, and re-layouts  8.96 us (13%)
  other arithmetic  6.67 us (9%)
  matrix products  3.58 us (5%)
    ppermute x13, waiting for transfers between devices, swap(): return lax.ppermute(value, axis, [(i, i ^ bit) for i in range(size)])  27 us
    ppermute x13, starting transfers between devices, swap(): return lax.ppermute(value, axis, [(i, i ^ bit) for i in range(size)])  14.9 us
    unnamed x12, local copies, waits for them, and re-layouts  2.56 us
    concatenate x2, local copies, waits for them, and re-layouts, ctx_gather(): return jnp.concatenate([mine, other], axis=dim)  1.9 us
    another operation x1, other arithmetic, per_device(): downs = jnp.stack([query_down, value_down], axis=1)  1.87 us
    dot_general x1, matrix products, per_device(): jnp.einsum('rd,sfkd->rfsk', tokens, down_half, preferred_element_type=jnp...  1.53 us
  transfers between devices with their start and end apart: 13, of which 5 were waited for; matrix products, arithmetic and copies ran while one was open for 20% of the time, Pallas kernels for 0%

profile of v3, /device:TPU:0, one launch (start us, length us, event | category | flops | bytes accessed | tf_op | source)
XLA Modules:
  0.0 70.9 jit_solution(9965413971528034812)
XLA Ops:
  0.0 3.0 %collective-permute-start.2 = (s32[1,2]{1,0:T(1,128)}, s32[1,2]{1,0:T(1,128)S(1)}, u32[]{:S(2)}, u32[]{:S(2)}) collective-permute-start(s32[1,2]{1,0:T(1,128)} %param.18), channel_id=1, source_target_pairs={{0,8},{4,12},{8,0},{12,4},{1,9},{5,13},{9,1},{13,5},{2,10},{6,14},... | collective-permute-start | bytes 32 | tf_op jit(solution)/shard_map/ppermute | solution.py:22
  3.0 1.6 %copy.18 = bf16[1,128,256]{1,2,0:T(8,128)(2,1)} copy(bf16[1,128,256]{2,1,0:T(8,128)(2,1)} %param.12) | data formatting | bytes 131072 | tf_op args[2]
  4.6 1.5 %collective-permute-start = (bf16[128,256]{0,1:T(8,128)(2,1)}, bf16[128,256]{0,1:T(8,128)(2,1)}, u32[]{:S(2)}, u32[]{:S(2)}) collective-permute-start(bf16[128,256]{0,1:T(8,128)(2,1)} %bitcast.2), channel_id=1, source_target_pairs={{0,16},{16,0},{1,17},{17,1},{2,18},{18,2},{3,19},{19,3},{4,20},{20... | collective-permute-start | bytes 196616 | tf_op jit(solution)/shard_map/ppermute | solution.py:22
  6.1 0.5 collective-permute-start.12
  6.6 1.0 %constant_dynamic-update-slice_fusion.1 = bf16[2,32,2304]{2,1,0:T(8,128)(2,1)S(1)} fusion(bf16[2,32,2048]{2,1,0:T(8,128)(2,1)} %param.15), kind=kLoop, calls=%fused_computation.77 | loop fusion | bytes 524288
  7.6 0.8 %constant_dynamic-update-slice_fusion = bf16[2,32,2304]{2,1,0:T(8,128)(2,1)S(1)} fusion(bf16[2,32,2304]{2,1,0:T(8,128)(2,1)S(1)} %constant_dynamic-update-slice_fusion.1, bf16[2,32,256]{2,1,0:T(8,128)(2,1)} %param.17), kind=kLoop, calls=%fused_computation.76 | loop fusion | bytes 65536 | tf_op jit(solution)/shard_map/concatenate | solution.py:159
  8.3 0.0 collective-permute-start.1
  8.3 1.9 %pad_maximum_fusion = bf16[2,2,32,2048]{3,2,1,0:T(8,128)(2,1)} fusion(bf16[2,1,32,2048]{3,2,1,0:T(8,128)(2,1)} %bitcast.82, bf16[2,1,32,2048]{3,2,1,0:T(8,128)(2,1)} %bitcast.79), kind=kLoop, calls=%fused_computation.24 | loop fusion | flops 262144 | bytes 1048576 | tf_op jit(solution)/shard_map/stack | solution.py:158
  10.2 0.5 collective-permute-start.5
  10.7 1.4 %fusion.50 = (s32[1,1]{1,0:T(1,128)}, s32[1,1]{1,0:T(1,128)}) fusion(s32[1,2]{1,0:T(1,128)} %param.18), kind=kLoop, calls=%fused_computation.87 | loop fusion | bytes 16 | tf_op jit(solution)/shard_map/slice | solution.py:77
  18.0 0.9 %copy.20 = bf16[128,2,128]{2,0,1:T(8,128)(2,1)S(1)} copy(bf16[128,2,128]{0,2,1:T(8,128)(2,1)} %bitcast.1) | data formatting | bytes 131072 | tf_op jit(solution)/shard_map/concatenate | solution.py:29
  19.0 0.1 bitcast_convert_fusion
  19.1 0.0 copy-start
  19.1 0.0 copy-start.1
  19.1 0.3 copy.22
  19.4 0.1 compare_and_fusion
  19.6 0.0 collective-permute-done.2
  19.6 1.6 %collective-permute-start.7 = (bf16[128,2048]{1,0:T(8,128)(2,1)}, bf16[128,2048]{1,0:T(8,128)(2,1)}, u32[]{:S(2)}, u32[]{:S(2)}) collective-permute-start(bf16[128,2048]{1,0:T(8,128)(2,1)} %bitcast.89), channel_id=1, source_target_pairs={{0,16},{16,0},{1,17},{17,1},{2,18},{18,2},{3,19},{19,3},{4,20},{20... | collective-permute-start | bytes 1572872 | tf_op jit(solution)/shard_map/ppermute | solution.py:22
  21.1 0.6 fusion.51
  25.4 0.0 collective-permute-done.1
  25.4 1.0 %dynamic-slice_select_fusion.1 = (bf16[1,32,2304]{2,1,0:T(8,128)(2,1)S(1)}, bf16[1,32,2304]{2,1,0:T(8,128)(2,1)S(1)}) fusion(bf16[2,32,2304]{2,1,0:T(8,128)(2,1)} %collective-permute-done.1, s32[]{:T(128)S(6)} %select_n.240, bf16[2,32,2304]{2,1,0:T(8,128)(2,1)S(1)} %constant_dynamic-update-slice_fusion, pred[]{:T(512)S(6)} %eq.52, s32[]{:T(128)S(6)} %select_n.246, ...), kind=kLoop, calls=%fused_computation.52 | loop fusion | flops 147456 | bytes 884746 | tf_op jit(solution)/shard_map/jit(_where)/select_n | solution.py:66
  26.4 0.6 collective-permute-start.3
  27.0 0.1 fusion.23
  27.1 0.0 copy-start.4
  27.1 0.1 pad_maximum_fusion.2
  27.2 1.6 %collective-permute-start.6 = (bf16[2,2,32,2048]{3,2,1,0:T(8,128)(2,1)S(1)}, bf16[2,2,32,2048]{3,2,1,0:T(8,128)(2,1)S(1)}, u32[]{:S(2)}, u32[]{:S(2)}) collective-permute-start(bf16[2,2,32,2048]{3,2,1,0:T(8,128)(2,1)S(1)} %pad_maximum_fusion.2), channel_id=1, source_target_pairs={{0,8},{4,12},{8,0},{12,4},{1,9},{5,13},{9,1},{13,5},{2,10},{6,14},... | collective-permute-start | bytes 1572872 | tf_op jit(solution)/shard_map/ppermute | solution.py:22
  28.8 7.6 %collective-permute-done.3 = bf16[2,32,2304]{2,1,0:T(8,128)(2,1)S(1)} collective-permute-done((bf16[2,32,2304]{2,1,0:T(8,128)(2,1)S(1)}, bf16[2,32,2304]{2,1,0:T(8,128)(2,1)S(1)}, u32[]{:S(2)}, u32[]{:S(2)}) %collective-permute-start.3) | collective-permute-done | bytes 294944 | tf_op jit(solution)/shard_map/ppermute | solution.py:22
  36.4 1.0 %slice_select_fusion.1 = (bf16[1,32,2304]{2,1,0:T(8,128)(2,1)S(1)}, bf16[1,32,2304]{2,1,0:T(8,128)(2,1)S(1)}) fusion(bf16[2,32,2304]{2,1,0:T(8,128)(2,1)S(1)} %collective-permute-done.3, bf16[2,32,2304]{2,1,0:T(8,128)(2,1)} %collective-permute-done.1, s32[]{:T(128)S(6)} %select_n.234, bf16[2,32,2304]{2,1,0:T(8,128)(2,1)S(1)} %constant_dynamic-update-slice_fusion, ...), kind=kLoop, calls=%fused_computation.50 | loop fusion | flops 294912 | bytes 1179660 | tf_op jit(solution)/shard_map/jit(_where)/select_n | solution.py:79
  37.4 9.0 %collective-permute-done.6 = bf16[2,2,32,2048]{3,2,1,0:T(8,128)(2,1)S(1)} collective-permute-done((bf16[2,2,32,2048]{3,2,1,0:T(8,128)(2,1)S(1)}, bf16[2,2,32,2048]{3,2,1,0:T(8,128)(2,1)S(1)}, u32[]{:S(2)}, u32[]{:S(2)}) %collective-permute-start.6) | collective-permute-done | bytes 524320 | tf_op jit(solution)/shard_map/ppermute | solution.py:22
  46.4 0.1 fusion.21
  46.5 0.0 copy-start.3
  46.5 1.5 %convolution_bitcast_fusion.2 = f32[256,2,2,32]{0,3,1,2:T(8,128)S(1)} fusion(bf16[128,2048]{1,0:T(8,128)(2,1)} %collective-permute-done.7, bf16[128,2048]{1,0:T(8,128)(2,1)S(1)} %bitcast.90, bf16[1,2,32,2048]{3,2,1,0:T(8,128)(2,1)S(1)} %get-tuple-element.28, bf16[1,2,32,2048]{3,2,1,0:T(8,128)(2,1)S(1)} %get-tuple-element.27), kind=kOutput, calls=%fused_computation.14 | convolution fusion | flops 136577024 | bytes 1703936 | tf_op jit(solution)/shard_map/rd,sfkd->rfsk/dot_general | solution.py:166
  48.0 3.7 %collective-permute-start.10 = (f32[256,2,2,32]{0,3,1,2:T(8,128)S(1)}, f32[256,2,2,32]{0,3,1,2:T(8,128)S(1)}, u32[]{:S(2)}, u32[]{:S(2)}) collective-permute-start(f32[256,2,2,32]{0,3,1,2:T(8,128)S(1)} %convolution_bitcast_fusion.2), channel_id=1, source_target_pairs={{0,3},{1,2},{2,1},{3,0},{4,7},{5,6},{6,5},{7,4},{8,11},{9,10},{10,... | collective-permute-start | bytes 393224 | tf_op jit(solution)/shard_map/ppermute | solution.py:22
  51.7 0.8 %collective-permute-start.8 = (f32[256,2,2,32]{0,3,1,2:T(8,128)S(1)}, f32[256,2,2,32]{0,3,1,2:T(8,128)S(1)}, u32[]{:S(2)}, u32[]{:S(2)}) collective-permute-start(f32[256,2,2,32]{0,3,1,2:T(8,128)S(1)} %convolution_bitcast_fusion.2), channel_id=1, source_target_pairs={{0,1},{1,0},{2,3},{3,2},{4,5},{5,4},{6,7},{7,6},{8,9},{9,8},{10,11... | collective-permute-start | bytes 393224 | tf_op jit(solution)/shard_map/ppermute | solution.py:22
  52.5 0.6 collective-permute-start.4
  53.1 0.9 %maximum_convert_fusion = f32[256,256]{1,0:T(8,128)S(1)} fusion(bf16[128,256]{1,0:T(8,128)(2,1)} %collective-permute-done.12, bf16[128,256]{1,0:T(8,128)(2,1)S(1)} %bitcast.88), kind=kLoop, calls=%fused_computation.56 | loop fusion | flops 262144 | bytes 393216 | tf_op jit(solution)/shard_map/convert_element_type | solution.py:197
  54.0 0.9 %copy.21 = bf16[128,2,128]{2,0,1:T(8,128)(2,1)S(1)} copy(bf16[128,2,128]{0,2,1:T(8,128)(2,1)} %bitcast.3) | data formatting | bytes 131072 | tf_op jit(solution)/shard_map/concatenate | solution.py:29
  55.0 0.1 copy.25
  55.1 1.2 %collective-permute-done.10 = f32[256,2,2,32]{0,3,1,2:T(8,128)S(1)} collective-permute-done((f32[256,2,2,32]{0,3,1,2:T(8,128)S(1)}, f32[256,2,2,32]{0,3,1,2:T(8,128)S(1)}, u32[]{:S(2)}, u32[]{:S(2)}) %collective-permute-start.10) | collective-permute-done | bytes 131104 | tf_op jit(solution)/shard_map/ppermute | solution.py:22
  56.3 5.5 %collective-permute-done.9 = f32[256,2,2,32]{0,3,1,2:T(8,128)S(1)} collective-permute-done((f32[256,2,2,32]{0,3,1,2:T(8,128)S(1)}, f32[256,2,2,32]{0,3,1,2:T(8,128)S(1)}, u32[]{:S(2)}, u32[]{:S(2)}) %collective-permute-start.9) | collective-permute-done | bytes 131104 | tf_op jit(solution)/shard_map/ppermute | solution.py:22
  61.8 0.6 collective-permute-start.11
  62.5 3.7 %collective-permute-done.11 = bf16[256,2,2,32]{0,3,1,2:T(8,128)(2,1)S(1)} collective-permute-done((bf16[256,2,2,32]{0,3,1,2:T(8,128)(2,1)S(1)}, bf16[256,2,2,32]{0,3,1,2:T(8,128)(2,1)S(1)}, u32[]{:S(2)}, u32[]{:S(2)}) %collective-permute-start.11) | collective-permute-done | bytes 65568 | tf_op jit(solution)/shard_map/ppermute | solution.py:22
  66.2 0.5 fusion.4
  66.7 0.7 %fusion = (f32[2,2,8,128]{3,2,0,1:T(8,128)S(1)}, f32[2,256,128,2,8]{2,1,4,3,0:T(8,128)S(1)}) fusion(pred[128,256]{0,1:T(8,128)(4,1)S(1)} %compare_and_fusion, bf16[128,2,2,8,128]{0,4,3,2,1:T(8,128)(2,1)S(1)} %bitcast.78, bf16[128,2,128]{2,0,1:T(8,128)(2,1)S(1)} %copy.21, bf16[128,2,128]{2,0,1:T(8,128)(2,1)S(1)} %copy.20), kind=kOutput, calls=%fused_computation.2 | convolution fusion | flops 271839232 | bytes 5423104 | tf_op jit(solution)/shard_map/while/body/eval_jaxpr/rsgjd,kgd->sgjrk/dot_general | solution.py:94
  67.5 1.3 %fusion.1 = (f32[2,2,8,128]{3,2,0,1:T(8,128)S(1)}, bf16[2,2,8,128,256]{3,4,2,0,1:T(8,128)(2,1)S(1)}) fusion(f32[2,256,128,2,8]{2,1,4,3,0:T(8,128)S(1)} %get-tuple-element.57, f32[2,2,8,128]{3,2,0,1:T(8,128)S(1)} %get-tuple-element.51, pred[128,256]{0,1:T(8,128)(4,1)S(1)} %compare_and_fusion), kind=kLoop, calls=%fused_computation.3 | loop fusion | flops 6287360 | bytes 6356992 | tf_op jit(solution)/shard_map/while/body/eval_jaxpr/reduce_sum | solution.py:106
  68.8 0.3 add_convert_fusion
  69.1 0.5 fusion.6
  69.6 1.3 %copy.28 = bf16[2,1,128,2048]{3,2,1,0:T(8,128)(2,1)} copy(bf16[2,1,128,2048]{2,3,0,1:T(8,128)(2,1)S(1)} %bitcast.85) | data formatting | bytes 2097152 | tf_op jit(solution)/shard_map/convert_element_type | solution.py:135
  (24 shorter events, 0.2 us)
Async XLA Ops:
  0.0 19.0 %copy-start.2 = (bf16[1,128,2048]{2,1,0:T(8,128)(2,1)S(1)}, bf16[1,128,2048]{2,1,0:T(8,128)(2,1)}, u32[]{:S(2)}) copy-start(bf16[1,128,2048]{2,1,0:T(8,128)(2,1)} %param.11) | copy-start | bytes 1572868
  0.0 19.6 %collective-permute-start.2 = (s32[1,2]{1,0:T(1,128)}, s32[1,2]{1,0:T(1,128)S(1)}, u32[]{:S(2)}, u32[]{:S(2)}) collective-permute-start(s32[1,2]{1,0:T(1,128)} %param.18), channel_id=1, source_target_pairs={{0,8},{4,12},{8,0},{12,4},{1,9},{5,13},{9,1},{13,5},{2,10},{6,14},... | collective-permute-start | bytes 32 | tf_op jit(solution)/shard_map/ppermute | solution.py:22
  4.6 49.4 %collective-permute-start = (bf16[128,256]{0,1:T(8,128)(2,1)}, bf16[128,256]{0,1:T(8,128)(2,1)}, u32[]{:S(2)}, u32[]{:S(2)}) collective-permute-start(bf16[128,256]{0,1:T(8,128)(2,1)} %bitcast.2), channel_id=1, source_target_pairs={{0,16},{16,0},{1,17},{17,1},{2,18},{18,2},{3,19},{19,3},{4,20},{20... | collective-permute-start | bytes 196616 | tf_op jit(solution)/shard_map/ppermute | solution.py:22
  6.1 46.5 %collective-permute-start.12 = (bf16[128,256]{1,0:T(8,128)(2,1)}, bf16[128,256]{1,0:T(8,128)(2,1)}, u32[]{:S(2)}, u32[]{:S(2)}) collective-permute-start(bf16[128,256]{1,0:T(8,128)(2,1)} %bitcast.87), channel_id=1, source_target_pairs={{0,16},{16,0},{1,17},{17,1},{2,18},{18,2},{3,19},{19,3},{4,20},{20... | collective-permute-start | bytes 196616 | tf_op jit(solution)/shard_map/ppermute | solution.py:22
  8.3 17.0 %collective-permute-start.1 = (bf16[2,32,2304]{2,1,0:T(8,128)(2,1)S(1)}, bf16[2,32,2304]{2,1,0:T(8,128)(2,1)}, u32[]{:S(2)}, u32[]{:S(2)}) collective-permute-start(bf16[2,32,2304]{2,1,0:T(8,128)(2,1)S(1)} %constant_dynamic-update-slice_fusion), channel_id=1, source_target_pairs={{0,4},{4,0},{8,12},{12,8},{1,5},{5,1},{9,13},{13,9},{2,6},{6,2},{1... | collective-permute-start | bytes 884744 | tf_op jit(solution)/shard_map/ppermute | solution.py:22
  10.2 16.8 %collective-permute-start.5 = (bf16[2,2,32,2048]{3,2,1,0:T(8,128)(2,1)}, bf16[2,2,32,2048]{3,2,1,0:T(8,128)(2,1)S(1)}, u32[]{:S(2)}, u32[]{:S(2)}) collective-permute-start(bf16[2,2,32,2048]{3,2,1,0:T(8,128)(2,1)} %pad_maximum_fusion), channel_id=1, source_target_pairs={{0,4},{4,0},{8,12},{12,8},{1,5},{5,1},{9,13},{13,9},{2,6},{6,2},{1... | collective-permute-start | bytes 1572872 | tf_op jit(solution)/shard_map/ppermute | solution.py:22
  19.1 7.9 %copy-start = (bf16[2,32,2048]{2,1,0:T(8,128)(2,1)S(1)}, bf16[2,32,2048]{2,1,0:T(8,128)(2,1)}, u32[]{:S(2)}) copy-start(bf16[2,32,2048]{2,1,0:T(8,128)(2,1)} %param.14) | copy-start | bytes 786436
  19.1 7.9 %copy-start.1 = (bf16[2,32,2048]{2,1,0:T(8,128)(2,1)S(1)}, bf16[2,32,2048]{2,1,0:T(8,128)(2,1)}, u32[]{:S(2)}) copy-start(bf16[2,32,2048]{2,1,0:T(8,128)(2,1)} %param.16) | copy-start | bytes 786436
  19.6 26.9 %collective-permute-start.7 = (bf16[128,2048]{1,0:T(8,128)(2,1)}, bf16[128,2048]{1,0:T(8,128)(2,1)}, u32[]{:S(2)}, u32[]{:S(2)}) collective-permute-start(bf16[128,2048]{1,0:T(8,128)(2,1)} %bitcast.89), channel_id=1, source_target_pairs={{0,16},{16,0},{1,17},{17,1},{2,18},{18,2},{3,19},{19,3},{4,20},{20... | collective-permute-start | bytes 1572872 | tf_op jit(solution)/shard_map/ppermute | solution.py:22
  26.4 9.9 %collective-permute-start.3 = (bf16[2,32,2304]{2,1,0:T(8,128)(2,1)S(1)}, bf16[2,32,2304]{2,1,0:T(8,128)(2,1)S(1)}, u32[]{:S(2)}, u32[]{:S(2)}) collective-permute-start(bf16[2,32,2304]{2,1,0:T(8,128)(2,1)S(1)} %pad_maximum_fusion.3), channel_id=1, source_target_pairs={{0,8},{4,12},{8,0},{12,4},{1,9},{5,13},{9,1},{13,5},{2,10},{6,14},... | collective-permute-start | bytes 884744 | tf_op jit(solution)/shard_map/ppermute | solution.py:22
  27.1 19.4 %copy-start.4 = (bf16[1,128,2048]{2,1,0:T(8,128)(2,1)S(1)}, bf16[1,128,2048]{2,1,0:T(8,128)(2,1)}, u32[]{:S(2)}) copy-start(bf16[1,128,2048]{2,1,0:T(8,128)(2,1)} %param.10) | copy-start | bytes 1572868
  27.2 19.2 %collective-permute-start.6 = (bf16[2,2,32,2048]{3,2,1,0:T(8,128)(2,1)S(1)}, bf16[2,2,32,2048]{3,2,1,0:T(8,128)(2,1)S(1)}, u32[]{:S(2)}, u32[]{:S(2)}) collective-permute-start(bf16[2,2,32,2048]{3,2,1,0:T(8,128)(2,1)S(1)} %pad_maximum_fusion.2), channel_id=1, source_target_pairs={{0,8},{4,12},{8,0},{12,4},{1,9},{5,13},{9,1},{13,5},{2,10},{6,14},... | collective-permute-start | bytes 1572872 | tf_op jit(solution)/shard_map/ppermute | solution.py:22
  46.5 6.7 %copy-start.3 = (bf16[1,128,256]{2,1,0:T(8,128)(2,1)S(1)}, bf16[1,128,256]{2,1,0:T(8,128)(2,1)}, u32[]{:S(2)}) copy-start(bf16[1,128,256]{2,1,0:T(8,128)(2,1)} %param.13) | copy-start | bytes 196612
  48.0 8.2 %collective-permute-start.10 = (f32[256,2,2,32]{0,3,1,2:T(8,128)S(1)}, f32[256,2,2,32]{0,3,1,2:T(8,128)S(1)}, u32[]{:S(2)}, u32[]{:S(2)}) collective-permute-start(f32[256,2,2,32]{0,3,1,2:T(8,128)S(1)} %convolution_bitcast_fusion.2), channel_id=1, source_target_pairs={{0,3},{1,2},{2,1},{3,0},{4,7},{5,6},{6,5},{7,4},{8,11},{9,10},{10,... | collective-permute-start | bytes 393224 | tf_op jit(solution)/shard_map/ppermute | solution.py:22
  51.7 10.1 %collective-permute-start.9 = (f32[256,2,2,32]{0,3,1,2:T(8,128)S(1)}, f32[256,2,2,32]{0,3,1,2:T(8,128)S(1)}, u32[]{:S(2)}, u32[]{:S(2)}) collective-permute-start(f32[256,2,2,32]{0,3,1,2:T(8,128)S(1)} %convolution_bitcast_fusion.2), channel_id=1, source_target_pairs={{0,2},{1,3},{2,0},{3,1},{4,6},{5,7},{6,4},{7,5},{8,10},{9,11},{10,... | collective-permute-start | bytes 393224 | tf_op jit(solution)/shard_map/ppermute | solution.py:22
  51.7 10.1 %collective-permute-start.8 = (f32[256,2,2,32]{0,3,1,2:T(8,128)S(1)}, f32[256,2,2,32]{0,3,1,2:T(8,128)S(1)}, u32[]{:S(2)}, u32[]{:S(2)}) collective-permute-start(f32[256,2,2,32]{0,3,1,2:T(8,128)S(1)} %convolution_bitcast_fusion.2), channel_id=1, source_target_pairs={{0,1},{1,0},{2,3},{3,2},{4,5},{5,4},{6,7},{7,6},{8,9},{9,8},{10,11... | collective-permute-start | bytes 393224 | tf_op jit(solution)/shard_map/ppermute | solution.py:22
  52.5 9.9 %collective-permute-start.4 = (bf16[2,32,2304]{2,1,0:T(8,128)(2,1)S(1)}, bf16[2,32,2304]{2,1,0:T(8,128)(2,1)S(1)}, u32[]{:S(2)}, u32[]{:S(2)}) collective-permute-start(bf16[2,32,2304]{2,1,0:T(8,128)(2,1)S(1)} %pad_maximum_fusion.4), channel_id=1, source_target_pairs={{0,16},{16,0},{1,17},{17,1},{2,18},{18,2},{3,19},{19,3},{4,20},{20... | collective-permute-start | bytes 884744 | tf_op jit(solution)/shard_map/ppermute | solution.py:22
  61.8 4.3 %collective-permute-start.11 = (bf16[256,2,2,32]{0,3,1,2:T(8,128)(2,1)S(1)}, bf16[256,2,2,32]{0,3,1,2:T(8,128)(2,1)S(1)}, u32[]{:S(2)}, u32[]{:S(2)}) collective-permute-start(bf16[256,2,2,32]{0,3,1,2:T(8,128)(2,1)S(1)} %add_convert_fusion.1), channel_id=1, source_target_pairs={{0,16},{16,0},{1,17},{17,1},{2,18},{18,2},{3,19},{19,3},{4,20},{20... | collective-permute-start | bytes 196616 | tf_op jit(solution)/shard_map/ppermute | solution.py:22
